TPU v7x, 32 devices: a whole 2x2x4 slice. The times are simulated.
32 devices in a mesh: dp: 2 (over core), expert: 16 (over z, y, x).
Axes of the slice: x: 2, y: 2, z: 4, core: 2. Of those that a mesh axis runs over, the one named last changes fastest.
Arguments:
- grad_out: bfloat16 [4096, 2048], P(('dp', 'expert')), may hold values from -0.59765625 to 0.59765625
- routes: int32 [4096, 8], P(('dp', 'expert')), may hold values from 0 to 15, all different within a row; in each aligned block of 128 rows (0 to 127, 128 to 255, ...) at most 96 rows name the same one
- router_probs: float32 [4096, 8], P(('dp', 'expert')), may hold values from 0.02 to 1
- saved_hidden: bfloat16 [16, 2, 1536, 768], P('expert', 'dp'), may hold values from -1.796875 to 1.796875
- down_weight: bfloat16 [16, 768, 2048], P('expert', 'dp'), may hold values from -0.21875 to 0.21875
- moment_one: bfloat16 [16, 768, 2048], P('expert', 'dp'), may hold values from -0.59765625 to 0.59765625
- moment_two: bfloat16 [16, 768, 2048], P('expert', 'dp'), may hold values from 0.0099487305 to 0.5
- partner: int32 [16], replicated, may hold values from 0 to 15, as said below
Outputs:
- gate_grad: float32 [4096, 8], P(('dp', 'expert'))
- new_down: bfloat16 [16, 768, 2048], P('expert', 'dp')
- new_moment_one: bfloat16 [16, 768, 2048], P('expert', 'dp')
- new_moment_two: bfloat16 [16, 768, 2048], P('expert', 'dp')
Inputs may be any that keep to these rules, and one draw needn't show every extreme that they name: `routes`: each row names 8 different experts. Among the 128 rows of one device no expert is named more than 96 times, and on some device an expert is named exactly 96 times. partner[partner[i]] = i, and partner[i] is either i or differs from i in exactly one bit.
All inputs are finite; a program needn't handle non-finite values.
Results may differ from a plain program's by a relative error of at most 0.0055.
Values may be sent and summed in bfloat16 or wider, within the bound.
No kernel may reach another device: no remote copies, remote signals or barrier semaphores. Data moves between devices by JAX's collectives and lax.ppermute only.
A program may use at most 128 MiB of HBM per device.

v0:
```python
import jax
import jax.numpy as jnp
from jax import lax
from jax.sharding import PartitionSpec as P

beta_one = 0.9
beta_two = 0.95
learn_rate = 0.001
weight_decay = 0.1
adam_epsilon = 1e-08
step_count = 1000


def adam_update(weight, moment_first, moment_second, grad_sum):
    first_new = beta_one * moment_first.astype(jnp.float32) + (1.0 - beta_one) * grad_sum
    second_new = (
        beta_two * moment_second.astype(jnp.float32) + (1.0 - beta_two) * grad_sum * grad_sum
    )
    corr_one = 1.0 - beta_one**step_count
    corr_two = 1.0 - beta_two**step_count
    weight_full = weight.astype(jnp.float32)
    direction = first_new / corr_one / (jnp.sqrt(second_new / corr_two) + adam_epsilon)
    updated = weight_full - learn_rate * (direction + weight_decay * weight_full)
    return (
        updated.astype(jnp.bfloat16),
        first_new.astype(jnp.bfloat16),
        second_new.astype(jnp.bfloat16),
    )


def route_table(expert_flat, partner):
    expert_iota = jnp.arange(partner.shape[0], dtype=jnp.int32)
    onehot = (expert_flat[:, None] == expert_iota[None, :]).astype(jnp.int32)
    pair_iota = jnp.arange(expert_flat.shape[0], dtype=jnp.int32)
    lower_ones = (pair_iota[:, None] >= pair_iota[None, :]).astype(jnp.bfloat16)
    running = jnp.dot(lower_ones, onehot.astype(jnp.bfloat16), preferred_element_type=jnp.float32)
    slot_rank = (jnp.sum(running * onehot.astype(jnp.float32), axis=1) - 1.0).astype(jnp.int32)
    mapped = jnp.sum(onehot * partner[None, :], axis=1)
    return (slot_rank, mapped)


def as_pieces(array, axis_size):
    return array.reshape(axis_size, array.size // axis_size)


def on_device(
    grad_out, routes, router_probs, saved_hidden, down_weight, moment_one, moment_two, partner
):
    tok_rows, top_count = routes.shape
    axis_size = lax.axis_size("expert")
    expert_count = partner.shape[0]
    capacity = 3 * tok_rows * top_count // (2 * expert_count)
    slot_count = capacity * axis_size
    pair_count = tok_rows * top_count
    expert_flat = routes.reshape(pair_count)
    slot_rank, mapped = route_table(expert_flat, partner)
    token_index = jnp.arange(pair_count, dtype=jnp.int32) // top_count
    prob_sum = jnp.sum(router_probs, axis=1, keepdims=True)
    gate_share = router_probs / prob_sum
    gate_low = gate_share.astype(jnp.bfloat16)
    weight = down_weight[0]
    moment_first = moment_one[0]
    moment_second = moment_two[0]
    hidden = saved_hidden[0, 0]
    slot_index = expert_flat * capacity + slot_rank
    token_of = jnp.zeros((slot_count,), jnp.int32).at[slot_index].set(token_index)
    filled = jnp.zeros((slot_count,), jnp.int32).at[slot_index].set(1)
    gate_of = (
        jnp.zeros((slot_count,), jnp.bfloat16).at[slot_index].set(gate_low.reshape(pair_count))
    )
    picked = grad_out[token_of]
    send_rows = jnp.where(filled[:, None] > 0, picked, jnp.zeros_like(picked))
    received, gate_in = (
        lax.all_to_all(send_rows, "expert", split_axis=0, concat_axis=0, tiled=True),
        lax.all_to_all(gate_of, "expert", split_axis=0, concat_axis=0, tiled=True),
    )
    scaled = gate_in[:, None] * received
    projected = lax.dot_general(
        received,
        lax.all_gather(weight, "dp", axis=0, tiled=True),
        (((1,), (1,)), ((), ())),
        preferred_element_type=jnp.float32,
    )
    products = jnp.sum(hidden.astype(jnp.float32) * projected, axis=1)
    grad_sum = lax.psum_scatter(
        lax.dot_general(
            hidden, scaled, (((0,), (0,)), ((), ())), preferred_element_type=jnp.float32
        ).astype(jnp.bfloat16),
        "dp",
        scatter_dimension=0,
        tiled=True,
    ).astype(jnp.float32)
    returned = lax.all_to_all(products, "expert", split_axis=0, concat_axis=0, tiled=True)
    answer = returned[slot_index].reshape(tok_rows, top_count)
    gate_grad = (answer - jnp.sum(gate_share * answer, axis=1, keepdims=True)) / prob_sum
    updated, first_new, second_new = adam_update(weight, moment_first, moment_second, grad_sum)
    outward = (
        lax.all_to_all(
            as_pieces(updated, axis_size), "expert", split_axis=0, concat_axis=0, tiled=True
        ),
        lax.all_to_all(
            as_pieces(first_new, axis_size), "expert", split_axis=0, concat_axis=0, tiled=True
        ),
        lax.all_to_all(
            as_pieces(second_new, axis_size), "expert", split_axis=0, concat_axis=0, tiled=True
        ),
    )
    turned_weight = jnp.take(outward[0], partner, axis=0)
    turned_first = jnp.take(outward[1], partner, axis=0)
    turned_second = jnp.take(outward[2], partner, axis=0)
    landed = (
        lax.all_to_all(turned_weight, "expert", split_axis=0, concat_axis=0, tiled=True),
        lax.all_to_all(turned_first, "expert", split_axis=0, concat_axis=0, tiled=True),
        lax.all_to_all(turned_second, "expert", split_axis=0, concat_axis=0, tiled=True),
    )
    new_down = landed[0].reshape(updated.shape)
    new_one = landed[1].reshape(first_new.shape)
    new_two = landed[2].reshape(second_new.shape)
    return (gate_grad, new_down[None], new_one[None], new_two[None])


def solution(mesh):
    in_specs = (
        P(("dp", "expert"), None),
        P(("dp", "expert"), None),
        P(("dp", "expert"), None),
        P("expert", "dp", None, None),
        P("expert", "dp", None),
        P("expert", "dp", None),
        P("expert", "dp", None),
        P(),
    )
    out_specs = (
        P(("dp", "expert"), None),
        P("expert", "dp", None),
        P("expert", "dp", None),
        P("expert", "dp", None),
    )
    return jax.shard_map(
        on_device, mesh=mesh, in_specs=in_specs, out_specs=out_specs, check_vma=False
    )
```

profile of v0, /device:TPU:0, one launch (start us, length us, event | category | flops | bytes accessed | tf_op | source)
XLA Modules:
  0.0 598.4 jit_solution(2959659223425681296)
XLA Ops:
  18.3 7.1 %gather_fusion = bf16[1536,2048]{1,0:T(8,128)(2,1)} fusion(bf16[128,2048]{1,0:T(8,128)(2,1)S(1)} %copy-done, s32[2048]{0:T(1024)S(1)} %pad_clamp_fusion), kind=kCustom, calls=%fused_computation.3 | custom fusion | bytes 12589056 | tf_op jit(solution)/shard_map/gather | solution.py:71
  31.4 8.5 %all-to-all-start = ((bf16[16,96,2048]{2,1,0:T(8,128)(2,1)}), bf16[16,96,2048]{2,1,0:T(8,128)(2,1)}, u32[]{:S(2)}, u32[]{:S(2)}) async-start(bf16[16,96,2048]{2,1,0:T(8,128)(2,1)} %broadcast_select_fusion), calls=%async_computation | async-start | bytes 12582912 | tf_op jit(solution)/shard_map/all_to_all | solution.py:74
  43.1 12.6 %all-gather.3.cloned.1.call-done = bf16[1,768,2048]{2,1,0:T(8,128)(2,1)} async-done(((bf16[1,384,2048]{2,1,0:T(8,128)(2,1)}), bf16[1,768,2048]{2,1,0:T(8,128)(2,1)}) %all-gather.3.cloned.1.call-update) | async-done | bytes 3145744 | tf_op jit(solution)/shard_map/all_gather | solution.py:80
  55.7 102.4 %all-to-all-done = bf16[16,96,2048]{2,1,0:T(8,128)(2,1)} async-done(((bf16[16,96,2048]{2,1,0:T(8,128)(2,1)}), bf16[16,96,2048]{2,1,0:T(8,128)(2,1)}, u32[]{:S(2)}, u32[]{:S(2)}) %all-to-all-start) | async-done | bytes 6291488 | tf_op jit(solution)/shard_map/all_to_all | solution.py:74
  158.1 8.5 %multiply_reduce_fusion = f32[1536]{0:T(1024)S(1)} fusion(bf16[1536,2048]{1,0:T(8,128)(2,1)} %bitcast.4, bf16[1,768,2048]{2,1,0:T(8,128)(2,1)} %all-gather.3.cloned.1.call-done, bf16[1,1,1536,768]{2,3,1,0:T(8,128)(2,1)} %copy.45), kind=kOutput, calls=%fused_computation.10 | convolution fusion | flops 4835375616 | bytes 11802624 | tf_op jit(solution)/shard_map/dot_general | solution.py:78
  167.3 29.9 %all-to-all-start.1 = ((f32[16,96,1]{1,2,0:T(1,128)}), f32[16,96,1]{1,2,0:T(1,128)S(1)}, u32[]{:S(2)}, u32[]{:S(2)}) async-start(f32[16,96,1]{1,2,0:T(1,128)} %bitcast.6), calls=%async_computation.1 | async-start | bytes 16384 | tf_op jit(solution)/shard_map/all_to_all | solution.py:93
  197.5 7.0 %all-to-all-done.1 = f32[16,96,1]{1,2,0:T(1,128)S(1)} async-done(((f32[16,96,1]{1,2,0:T(1,128)}), f32[16,96,1]{1,2,0:T(1,128)S(1)}, u32[]{:S(2)}, u32[]{:S(2)}) %all-to-all-start.1) | async-done | bytes 6176 | tf_op jit(solution)/shard_map/all_to_all | solution.py:93
  205.7 6.1 %gather_fusion.1 = f32[1024]{0:T(1024)S(1)} fusion(f32[1536]{0:T(1024)S(1)} %all_to_all.66, s32[1024]{0:T(1024)S(1)} %broadcast_clamp_fusion), kind=kCustom, calls=%fused_computation.4 | custom fusion | bytes 12288 | tf_op jit(solution)/shard_map/gather | solution.py:94
  212.3 7.6 %scatter_custom_fusion.2 = bf16[1536]{0:T(1024)(128)(2,1)S(1)} fusion(s32[1024]{0:T(1024)S(1)} %bitcast.62, bf16[1024]{0:T(1024)(128)(2,1)S(1)} %reshape.171, bf16[]{:T(256)} %constant.19.clone.1), kind=kCustom, calls=%fused_computation.64 | custom fusion | bytes 3074 | tf_op jit(solution)/shard_map/scatter | solution.py:69
  220.0 10.1 %all_to_all.97 = bf16[16,96,1]{1,2,0:T(2,128)(2,1)S(1)} all-to-all(bf16[16,96,1]{1,2,0:T(2,128)(2,1)S(1)} %all_to_all.84), channel_id=1, replica_groups=mesh['dp'=2,'expert'=16] {'expert'}, dimensions={0} | all-to-all | bytes 6144 | tf_op jit(solution)/shard_map/all_to_all | solution.py:75
  266.6 11.4 %reduce.7 = bf16[16,49152]{1,0:T(8,128)(2,1)} reduce(bf16[16,1,49152]{2,1,0:T(2,128)(2,1)S(1)} %all_to_all.87, bf16[]{:T(256)} %broadcast.152), dimensions={1}, to_apply=%all_to_all.87.reduce_sub_computation | reduce | bytes 3145730 | tf_op jit(solution)/shard_map/all_to_all | solution.py:104
  281.3 7.1 %all-to-all-start.7 = ((bf16[16,2,24576]{2,1,0:T(2,128)(2,1)}), bf16[16,2,24576]{2,1,0:T(2,128)(2,1)}, u32[]{:S(2)}, u32[]{:S(2)}) async-start(bf16[16,2,24576]{2,1,0:T(2,128)(2,1)} %reshape.215), calls=%async_computation.7 | async-start | bytes 3145728 | tf_op jit(solution)/shard_map/all_to_all | solution.py:104
  295.4 11.4 %reduce.8 = bf16[16,49152]{1,0:T(8,128)(2,1)} reduce(bf16[16,1,49152]{2,1,0:T(2,128)(2,1)S(1)} %all_to_all.86, bf16[]{:T(256)} %broadcast.152), dimensions={1}, to_apply=%all_to_all.86.reduce_sub_computation | reduce | bytes 3145730 | tf_op jit(solution)/shard_map/all_to_all | solution.py:101
  310.0 12.7 %all-to-all-done.7 = bf16[16,2,24576]{2,1,0:T(2,128)(2,1)} async-done(((bf16[16,2,24576]{2,1,0:T(2,128)(2,1)}), bf16[16,2,24576]{2,1,0:T(2,128)(2,1)}, u32[]{:S(2)}, u32[]{:S(2)}) %all-to-all-start.7) | async-done | bytes 1572896 | tf_op jit(solution)/shard_map/all_to_all | solution.py:104
  322.7 8.5 %all-to-all-start.5 = ((bf16[16,2,24576]{2,1,0:T(2,128)(2,1)}), bf16[16,2,24576]{2,1,0:T(2,128)(2,1)}, u32[]{:S(2)}, u32[]{:S(2)}) async-start(bf16[16,2,24576]{2,1,0:T(2,128)(2,1)} %reshape.211), calls=%async_computation.5 | async-start | bytes 3145728 | tf_op jit(solution)/shard_map/all_to_all | solution.py:101
  338.1 11.4 %reduce.9 = bf16[16,49152]{1,0:T(8,128)(2,1)} reduce(bf16[16,1,49152]{2,1,0:T(2,128)(2,1)S(1)} %all_to_all.85, bf16[]{:T(256)} %broadcast.152), dimensions={1}, to_apply=%all_to_all.85.reduce_sub_computation | reduce | bytes 3145730 | tf_op jit(solution)/shard_map/all_to_all | solution.py:98
  352.8 12.1 %all-to-all-done.5 = bf16[16,2,24576]{2,1,0:T(2,128)(2,1)} async-done(((bf16[16,2,24576]{2,1,0:T(2,128)(2,1)}), bf16[16,2,24576]{2,1,0:T(2,128)(2,1)}, u32[]{:S(2)}, u32[]{:S(2)}) %all-to-all-start.5) | async-done | bytes 1572896 | tf_op jit(solution)/shard_map/all_to_all | solution.py:101
  364.9 7.8 %all-to-all-start.3 = ((bf16[16,2,24576]{2,1,0:T(2,128)(2,1)}), bf16[16,2,24576]{2,1,0:T(2,128)(2,1)}, u32[]{:S(2)}, u32[]{:S(2)}) async-start(bf16[16,2,24576]{2,1,0:T(2,128)(2,1)} %reshape.207), calls=%async_computation.3 | async-start | bytes 3145728 | tf_op jit(solution)/shard_map/all_to_all | solution.py:98
  372.7 10.0 %reshape.216 = bf16[16,1,49152]{2,1,0:T(2,128)(2,1)} reshape(bf16[16,2,24576]{2,1,0:T(2,128)(2,1)} %all-to-all-done.7) | data formatting | bytes 3145728
  386.3 10.0 %reshape.212 = bf16[16,1,49152]{2,1,0:T(2,128)(2,1)} reshape(bf16[16,2,24576]{2,1,0:T(2,128)(2,1)} %all-to-all-done.5) | data formatting | bytes 3145728
  406.2 10.0 %reshape.208 = bf16[16,1,49152]{2,1,0:T(2,128)(2,1)} reshape(bf16[16,2,24576]{2,1,0:T(2,128)(2,1)} %all-to-all-done.3) | data formatting | bytes 3145728
  433.7 7.4 %all-to-all-start.4 = ((bf16[16,2,24576]{2,1,0:T(2,128)(2,1)}), bf16[16,2,24576]{2,1,0:T(2,128)(2,1)}, u32[]{:S(2)}, u32[]{:S(2)}) async-start(bf16[16,2,24576]{2,1,0:T(2,128)(2,1)} %reshape.209), calls=%async_computation.4 | async-start | bytes 3145728 | tf_op jit(solution)/shard_map/all_to_all | solution.py:112
  446.9 27.8 %all-to-all-done.4 = bf16[16,2,24576]{2,1,0:T(2,128)(2,1)} async-done(((bf16[16,2,24576]{2,1,0:T(2,128)(2,1)}), bf16[16,2,24576]{2,1,0:T(2,128)(2,1)}, u32[]{:S(2)}, u32[]{:S(2)}) %all-to-all-start.4) | async-done | bytes 1572896 | tf_op jit(solution)/shard_map/all_to_all | solution.py:112
  474.7 7.4 %all-to-all-start.6 = ((bf16[16,2,24576]{2,1,0:T(2,128)(2,1)}), bf16[16,2,24576]{2,1,0:T(2,128)(2,1)S(1)}, u32[]{:S(2)}, u32[]{:S(2)}) async-start(bf16[16,2,24576]{2,1,0:T(2,128)(2,1)} %reshape.213), calls=%async_computation.6 | async-start | bytes 3145728 | tf_op jit(solution)/shard_map/all_to_all | solution.py:113
  487.9 27.7 %all-to-all-done.6 = bf16[16,2,24576]{2,1,0:T(2,128)(2,1)S(1)} async-done(((bf16[16,2,24576]{2,1,0:T(2,128)(2,1)}), bf16[16,2,24576]{2,1,0:T(2,128)(2,1)S(1)}, u32[]{:S(2)}, u32[]{:S(2)}) %all-to-all-start.6) | async-done | bytes 1572896 | tf_op jit(solution)/shard_map/all_to_all | solution.py:113
  516.7 7.3 %all-to-all-start.8 = ((bf16[16,2,24576]{2,1,0:T(2,128)(2,1)}), bf16[16,2,24576]{2,1,0:T(2,128)(2,1)}, u32[]{:S(2)}, u32[]{:S(2)}) async-start(bf16[16,2,24576]{2,1,0:T(2,128)(2,1)} %reshape.217), calls=%async_computation.8 | async-start | bytes 3145728 | tf_op jit(solution)/shard_map/all_to_all | solution.py:114
  524.8 8.1 %reshape.210 = bf16[16,1,49152]{2,1,0:T(2,128)(2,1)S(1)} reshape(bf16[16,2,24576]{2,1,0:T(2,128)(2,1)} %all-to-all-done.4) | data formatting | bytes 3145728
  532.9 10.7 %reduce.1 = bf16[16,49152]{1,0:T(8,128)(2,1)} reduce(bf16[16,1,49152]{2,1,0:T(2,128)(2,1)S(1)} %reshape.210, bf16[]{:T(256)} %constant.64), dimensions={1}, to_apply=%all_to_all.73.reduce_sub_computation | reduce | bytes 3145730 | tf_op jit(solution)/shard_map/all_to_all | solution.py:112
  546.4 8.3 %reshape.214 = bf16[16,1,49152]{2,1,0:T(2,128)(2,1)S(1)} reshape(bf16[16,2,24576]{2,1,0:T(2,128)(2,1)} %copy-done.3) | data formatting | bytes 3145728
  554.7 10.7 %reduce.2 = bf16[16,49152]{1,0:T(8,128)(2,1)} reduce(bf16[16,1,49152]{2,1,0:T(2,128)(2,1)S(1)} %reshape.214, bf16[]{:T(256)} %constant.64), dimensions={1}, to_apply=%all_to_all.78.reduce_sub_computation | reduce | bytes 3145730 | tf_op jit(solution)/shard_map/all_to_all | solution.py:113
  568.2 10.2 %reshape.218 = bf16[16,1,49152]{2,1,0:T(2,128)(2,1)} reshape(bf16[16,2,24576]{2,1,0:T(2,128)(2,1)} %all-to-all-done.8) | data formatting | bytes 3145728
  578.4 11.1 %reduce.3 = bf16[16,49152]{1,0:T(8,128)(2,1)S(1)} reduce(bf16[16,1,49152]{2,1,0:T(2,128)(2,1)} %reshape.218, bf16[]{:T(256)} %constant.64), dimensions={1}, to_apply=%all_to_all.83.reduce_sub_computation | reduce | bytes 3145730 | tf_op jit(solution)/shard_map/all_to_all | solution.py:114
  (96 shorter events, 134.8 us)
Async XLA Ops:
  7.2 11.2 %copy-start = (bf16[128,2048]{1,0:T(8,128)(2,1)S(1)}, bf16[128,2048]{1,0:T(8,128)(2,1)}, u32[]{:S(2)}) copy-start(bf16[128,2048]{1,0:T(8,128)(2,1)} %param.10) | copy-start | bytes 1572868
  31.4 9.2 %copy-start.6 = (bf16[1,1,1536,768]{3,2,1,0:T(8,128)(2,1)S(1)}, bf16[1,1,1536,768]{3,2,1,0:T(8,128)(2,1)}, u32[]{:S(2)}) copy-start(bf16[1,1,1536,768]{3,2,1,0:T(8,128)(2,1)} %param.13) | copy-start | bytes 7077892
  31.4 126.7 %all-to-all-start = ((bf16[16,96,2048]{2,1,0:T(8,128)(2,1)}), bf16[16,96,2048]{2,1,0:T(8,128)(2,1)}, u32[]{:S(2)}, u32[]{:S(2)}) async-start(bf16[16,96,2048]{2,1,0:T(8,128)(2,1)} %broadcast_select_fusion), calls=%async_computation | async-start | bytes 12582912 | tf_op jit(solution)/shard_map/all_to_all | solution.py:74
  39.9 15.8 %all-gather.3.cloned.1.call-start = ((), (), s32[]{:S(2)}) async-start(), calls=%async_computation.10 | async-start | bytes 4718592 | tf_op jit(solution)/shard_map/all_gather | solution.py:80
  158.1 39.2 %copy-start.8 = (f32[128,8]{0,1:T(8,128)S(1)}, f32[128,8]{0,1:T(8,128)}, u32[]{:S(2)}) copy-start(f32[128,8]{0,1:T(8,128)} %param.12) | copy-start | bytes 12292
  167.3 37.1 %all-to-all-start.1 = ((f32[16,96,1]{1,2,0:T(1,128)}), f32[16,96,1]{1,2,0:T(1,128)S(1)}, u32[]{:S(2)}, u32[]{:S(2)}) async-start(f32[16,96,1]{1,2,0:T(1,128)} %bitcast.6), calls=%async_computation.1 | async-start | bytes 16384 | tf_op jit(solution)/shard_map/all_to_all | solution.py:93
  197.3 52.2 %reduce-scatter.4.cloned.1.call-start = ((), (), s32[]{:S(2)}) async-start(), calls=%async_computation.11 | async-start | bytes 4718592
  230.0 3.5 copy-start.7
  242.0 1.4 copy-start.2
  281.3 7.1 %copy-start.5 = (bf16[384,2048]{0,1:T(8,128)(2,1)S(1)}, bf16[384,2048]{0,1:T(8,128)(2,1)}, u32[]{:S(2)}) copy-start(bf16[384,2048]{0,1:T(8,128)(2,1)} %get-tuple-element.19) | copy-start | bytes 4718596
  281.3 41.4 %all-to-all-start.7 = ((bf16[16,2,24576]{2,1,0:T(2,128)(2,1)}), bf16[16,2,24576]{2,1,0:T(2,128)(2,1)}, u32[]{:S(2)}, u32[]{:S(2)}) async-start(bf16[16,2,24576]{2,1,0:T(2,128)(2,1)} %reshape.215), calls=%async_computation.7 | async-start | bytes 3145728 | tf_op jit(solution)/shard_map/all_to_all | solution.py:104
  310.0 21.1 %copy-start.4 = (bf16[384,2048]{0,1:T(8,128)(2,1)S(1)}, bf16[384,2048]{0,1:T(8,128)(2,1)}, u32[]{:S(2)}) copy-start(bf16[384,2048]{0,1:T(8,128)(2,1)} %get-tuple-element.18) | copy-start | bytes 4718596
  322.7 42.2 %all-to-all-start.5 = ((bf16[16,2,24576]{2,1,0:T(2,128)(2,1)}), bf16[16,2,24576]{2,1,0:T(2,128)(2,1)}, u32[]{:S(2)}, u32[]{:S(2)}) async-start(bf16[16,2,24576]{2,1,0:T(2,128)(2,1)} %reshape.211), calls=%async_computation.5 | async-start | bytes 3145728 | tf_op jit(solution)/shard_map/all_to_all | solution.py:101
  352.8 19.8 %copy-start.9 = (s32[16]{0:T(128)S(1)}, s32[16]{0:T(128)}, u32[]{:S(2)}) copy-start(s32[16]{0:T(128)} %param.17) | copy-start | bytes 196
  364.9 41.4 %all-to-all-start.3 = ((bf16[16,2,24576]{2,1,0:T(2,128)(2,1)}), bf16[16,2,24576]{2,1,0:T(2,128)(2,1)}, u32[]{:S(2)}, u32[]{:S(2)}) async-start(bf16[16,2,24576]{2,1,0:T(2,128)(2,1)} %reshape.207), calls=%async_computation.3 | async-start | bytes 3145728 | tf_op jit(solution)/shard_map/all_to_all | solution.py:98
  433.7 40.9 %all-to-all-start.4 = ((bf16[16,2,24576]{2,1,0:T(2,128)(2,1)}), bf16[16,2,24576]{2,1,0:T(2,128)(2,1)}, u32[]{:S(2)}, u32[]{:S(2)}) async-start(bf16[16,2,24576]{2,1,0:T(2,128)(2,1)} %reshape.209), calls=%async_computation.4 | async-start | bytes 3145728 | tf_op jit(solution)/shard_map/all_to_all | solution.py:112
  474.7 40.9 %all-to-all-start.6 = ((bf16[16,2,24576]{2,1,0:T(2,128)(2,1)}), bf16[16,2,24576]{2,1,0:T(2,128)(2,1)S(1)}, u32[]{:S(2)}, u32[]{:S(2)}) async-start(bf16[16,2,24576]{2,1,0:T(2,128)(2,1)} %reshape.213), calls=%async_computation.6 | async-start | bytes 3145728 | tf_op jit(solution)/shard_map/all_to_all | solution.py:113
  515.6 1.1 copy-start.3
  516.7 51.4 %all-to-all-start.8 = ((bf16[16,2,24576]{2,1,0:T(2,128)(2,1)}), bf16[16,2,24576]{2,1,0:T(2,128)(2,1)}, u32[]{:S(2)}, u32[]{:S(2)}) async-start(bf16[16,2,24576]{2,1,0:T(2,128)(2,1)} %reshape.217), calls=%async_computation.8 | async-start | bytes 3145728 | tf_op jit(solution)/shard_map/all_to_all | solution.py:114
  578.4 12.8 %copy-start.1 = (bf16[128,2048]{1,0:T(8,128)(2,1)S(1)}, bf16[128,2048]{1,0:T(8,128)(2,1)}, u32[]{:S(2)}) copy-start(bf16[128,2048]{1,0:T(8,128)(2,1)} %param.10) | copy-start | bytes 1572868
Sparse Core Ops, SparseCore 0:
  42.2 13.3 all-gather.2
  242.2 7.2 reduce-scatter.3
where the time goes:
time: 611 us; the launch traced here: 598 us
  waiting for transfers between devices  204 us (33%)
  local copies, waits for them, and re-layouts  174 us (28%)
  other arithmetic  96.3 us (16%)
  starting transfers between devices  84 us (14%)
  between operations  14.9 us (2%)
  matrix products  14.6 us (2%)
  blocking collectives  10.1 us (2%)
    unnamed x45, local copies, waits for them, and re-layouts  105 us
    all_to_all x1, waiting for transfers between devices, on_device(): lax.all_to_all(send_rows, 'expert', split_axis=0, concat_axis=0, tiled=True)  102 us
    all_to_all x1, starting transfers between devices, on_device(): lax.all_to_all(products, 'expert', split_axis=0, concat_axis=0, tiled=True)  29.9 us
    all_to_all x1, waiting for transfers between devices, on_device(): lax.all_to_all(turned_weight, 'expert', split_axis=0, concat_axis=0, tile...  27.8 us
    all_to_all x1, waiting for transfers between devices, on_device(): lax.all_to_all(turned_first, 'expert', split_axis=0, concat_axis=0, tiled...  27.7 us
    all_to_all x3, other arithmetic, on_device(): lax.all_to_all(turned_second, 'expert', split_axis=0, concat_axis=0, tile...  17.6 us
    all_to_all x2, other arithmetic, on_device(): lax.all_to_all(turned_weight, 'expert', split_axis=0, concat_axis=0, tile...  14.6 us
    all_to_all x2, other arithmetic, on_device(): lax.all_to_all(turned_first, 'expert', split_axis=0, concat_axis=0, tiled...  13.2 us
  transfers between devices with their start and end apart: 10, of which 9 were waited for; matrix products, arithmetic and copies ran while one was open for 22% of the time, Pallas kernels for 0%

commit v1 on v0

v1 whole, which is shorter than its diff:
```python
import jax
import jax.numpy as jnp
from jax import lax
from jax.sharding import PartitionSpec as P

beta_one = 0.9
beta_two = 0.95
learn_rate = 0.001
weight_decay = 0.1
adam_epsilon = 1e-08
step_count = 1000

gather_limit_bytes = 16 * 1024 * 1024


def adam_update(weight, moment_first, moment_second, grad_sum):
    first_new = beta_one * moment_first.astype(jnp.float32) + (1.0 - beta_one) * grad_sum
    second_new = (
        beta_two * moment_second.astype(jnp.float32) + (1.0 - beta_two) * grad_sum * grad_sum
    )
    corr_one = 1.0 - beta_one**step_count
    corr_two = 1.0 - beta_two**step_count
    weight_full = weight.astype(jnp.float32)
    direction = first_new / corr_one / (jnp.sqrt(second_new / corr_two) + adam_epsilon)
    updated = weight_full - learn_rate * (direction + weight_decay * weight_full)
    return (
        updated.astype(jnp.bfloat16),
        first_new.astype(jnp.bfloat16),
        second_new.astype(jnp.bfloat16),
    )


def block_ranks(hit):
    return jnp.cumsum(hit.astype(jnp.int32), axis=-1) - 1


def slot_onehot(hit, rank, capacity):
    slot_iota = jnp.arange(capacity, dtype=jnp.int32)
    return hit[..., None, :] & (rank[..., None, :] == slot_iota[:, None])


def on_device(
    grad_out, routes, router_probs, saved_hidden, down_weight, moment_one, moment_two, partner
):
    tok_rows, top_count = routes.shape
    width = grad_out.shape[1]
    axis_size = lax.axis_size("expert")
    me = lax.axis_index("expert")
    expert_count = partner.shape[0]
    capacity = 3 * tok_rows * top_count // (2 * expert_count)
    slot_count = capacity * axis_size

    weight = down_weight[0]
    weight_full = lax.all_gather(weight, "dp", axis=0, tiled=True)
    hidden = saved_hidden[0, 0]

    prob_sum = jnp.sum(router_probs, axis=1, keepdims=True)
    gate_share = router_probs / prob_sum
    gate_low = gate_share.astype(jnp.bfloat16)

    expert_iota = jnp.arange(expert_count, dtype=jnp.int32)
    local_hit = jnp.any(routes[:, :, None] == expert_iota[None, None, :], axis=1)
    local_rank = block_ranks(local_hit.T).T
    pair_rank = jnp.take_along_axis(local_rank, routes, axis=1)

    gather_bytes = axis_size * tok_rows * width * grad_out.dtype.itemsize
    if gather_bytes <= gather_limit_bytes:
        packed = jnp.concatenate([routes.astype(jnp.float32), router_probs], axis=1)
        packed_all = lax.all_gather(packed, "expert", axis=0, tiled=True)
        grad_all = lax.all_gather(grad_out, "expert", axis=0, tiled=True)
        routes_all = packed_all[:, :top_count].astype(jnp.int32)
        probs_all = packed_all[:, top_count:]
        gate_all = (probs_all / jnp.sum(probs_all, axis=1, keepdims=True)).astype(jnp.bfloat16)
        hit_k = routes_all == me
        hit = jnp.any(hit_k, axis=1).reshape(axis_size, tok_rows)
        gate_tok = jnp.sum(
            jnp.where(hit_k, gate_all.astype(jnp.float32), 0.0), axis=1
        ).reshape(axis_size, tok_rows)
        onehot = slot_onehot(hit, block_ranks(hit), capacity)
        dispatched = jnp.einsum(
            "sjt,std->sjd",
            onehot.astype(jnp.bfloat16),
            grad_all.reshape(axis_size, tok_rows, width),
            preferred_element_type=jnp.float32,
        ).astype(jnp.bfloat16)
        slot_gate = jnp.sum(
            jnp.where(onehot, gate_tok[:, None, :], 0.0), axis=2
        ).astype(jnp.bfloat16)
    else:
        gate_pair = jnp.sum(
            jnp.where(
                routes[:, :, None] == expert_iota[None, None, :],
                gate_low.astype(jnp.float32)[:, :, None],
                0.0,
            ),
            axis=1,
        )
        onehot = slot_onehot(local_hit.T, local_rank.T, capacity)
        send_rows = jnp.einsum(
            "ejt,td->ejd",
            onehot.astype(jnp.bfloat16),
            grad_out,
            preferred_element_type=jnp.float32,
        ).astype(jnp.bfloat16)
        send_gate = jnp.sum(jnp.where(onehot, gate_pair.T[:, None, :], 0.0), axis=2).astype(
            jnp.bfloat16
        )
        dispatched = lax.all_to_all(send_rows, "expert", split_axis=0, concat_axis=0, tiled=True)
        slot_gate = lax.all_to_all(send_gate, "expert", split_axis=0, concat_axis=0, tiled=True)

    dispatched = dispatched.reshape(slot_count, width)
    slot_gate = slot_gate.reshape(slot_count)
    scaled = slot_gate[:, None] * dispatched
    projected = lax.dot_general(
        dispatched,
        weight_full,
        (((1,), (1,)), ((), ())),
        preferred_element_type=jnp.float32,
    )
    products = jnp.sum(hidden.astype(jnp.float32) * projected, axis=1)
    grad_sum = lax.psum_scatter(
        lax.dot_general(
            hidden, scaled, (((0,), (0,)), ((), ())), preferred_element_type=jnp.float32
        ).astype(jnp.bfloat16),
        "dp",
        scatter_dimension=0,
        tiled=True,
    ).astype(jnp.float32)
    returned = lax.all_to_all(
        products.reshape(axis_size, capacity), "expert", split_axis=0, concat_axis=0, tiled=True
    )
    answer = returned.reshape(-1)[routes * capacity + pair_rank]
    gate_grad = (answer - jnp.sum(gate_share * answer, axis=1, keepdims=True)) / prob_sum

    outputs = adam_update(weight, moment_one[0], moment_two[0], grad_sum)

    mine = partner[me]
    levels = axis_size.bit_length() - 1
    which = jnp.int32(0)
    cases = [outputs]
    for level in range(levels):
        flip = 1 << level
        which = which + jnp.where(mine == (me ^ flip), level + 1, 0).astype(jnp.int32)
        cases.append(
            lax.ppermute(outputs, "expert", perm=[(i, i ^ flip) for i in range(axis_size)])
        )
    landed = [
        lax.select_n(which, *[case[index] for case in cases]) for index in range(3)
    ]
    return (gate_grad, landed[0][None], landed[1][None], landed[2][None])


def solution(mesh):
    in_specs = (
        P(("dp", "expert"), None),
        P(("dp", "expert"), None),
        P(("dp", "expert"), None),
        P("expert", "dp", None, None),
        P("expert", "dp", None),
        P("expert", "dp", None),
        P("expert", "dp", None),
        P(),
    )
    out_specs = (
        P(("dp", "expert"), None),
        P("expert", "dp", None),
        P("expert", "dp", None),
        P("expert", "dp", None),
    )
    return jax.shard_map(
        on_device, mesh=mesh, in_specs=in_specs, out_specs=out_specs, check_vma=False
    )
```

time: 611 us -> 394 us (0.64)
  the two profiles are of different devices: /device:TPU:0 before, /device:TPU:8 now
where the time goes in v1:
time: 394 us; the launch traced here: 389 us
  waiting for transfers between devices  240 us (61%)
  local copies, waits for them, and re-layouts  36.5 us (9%)
  blocking collectives  36.1 us (9%)
  matrix products  22.1 us (6%)
  starting transfers between devices  21.3 us (5%)
  other arithmetic  16.7 us (4%)
  between operations  16.5 us (4%)
    ppermute x12, waiting for transfers between devices, on_device(): lax.ppermute(outputs, 'expert', perm=[(i, i ^ flip) for i in range(axis_s...  114 us
    all_gather x1, waiting for transfers between devices, on_device(): grad_all = lax.all_gather(grad_out, 'expert', axis=0, tiled=True)  70.5 us
    all_to_all x1, waiting for transfers between devices, on_device(): lax.all_to_all(products.reshape(axis_size, capacity), 'expert', split_axi...  49.8 us
    all_gather x1, blocking collectives, on_device(): packed_all = lax.all_gather(packed, 'expert', axis=0, tiled=True)  36.1 us
    unnamed x28, local copies, waits for them, and re-layouts  20.8 us
    ppermute x12, starting transfers between devices, on_device(): lax.ppermute(outputs, 'expert', perm=[(i, i ^ flip) for i in range(axis_s...  17.3 us
    dot_general x1, matrix products, on_device(): lax.dot_general(dispatched, weight_full, (((1,), (1,)), ((), ())), prefer...  8.55 us
    dot_general x1, matrix products, on_device(): jnp.einsum('sjt,std->sjd', onehot.astype(jnp.bfloat16), grad_all.reshape(...  7.98 us
  transfers between devices with their start and end apart: 16, of which 8 were waited for; matrix products, arithmetic and copies ran while one was open for 14% of the time, Pallas kernels for 0%

profile of v1, /device:TPU:8, one launch (start us, length us, event | category | flops | bytes accessed | tf_op | source)
XLA Modules:
  0.0 389.3 jit_solution(13495440133207266808)
XLA Ops:
  9.9 7.0 %gather_fusion.1 = s32[1024]{0:T(1024)S(1)} fusion(s32[128,16]{0,1:T(8,128)S(1)} %add_bitcast_fusion, s32[1024]{0:T(1024)S(1)} %reshape.77), kind=kCustom, calls=%fused_computation.1 | custom fusion | bytes 16384 | tf_op jit(solution)/shard_map/jit(take_along_axis)/gather | solution.py:64
  17.1 36.1 %all_gather.9 = f32[2048,16]{0,1:T(8,128)S(1)} all-gather(f32[128,16]{0,1:T(8,128)S(1)} %pad_maximum_fusion), channel_id=1, replica_groups=mesh['dp'=2,'expert'=16] {'expert'}, dimensions={0}, use_global_device_ids=true | all-gather | bytes 139264 | tf_op jit(solution)/shard_map/all_gather | solution.py:69
  53.9 70.5 %all-gather.4.cloned.1.call-done = bf16[2048,2048]{1,0:T(8,128)(2,1)} async-done(((bf16[128,2048]{1,0:T(8,128)(2,1)}), bf16[2048,2048]{1,0:T(8,128)(2,1)}) %all-gather.4.cloned.1.call-update) | async-done | bytes 8388624 | tf_op jit(solution)/shard_map/all_gather | solution.py:70
  124.4 8.0 %broadcast_multiply_fusion = (bf16[16,96,2048]{2,1,0:T(8,128)(2,1)S(1)}, bf16[16,96,2048]{2,1,0:T(8,128)(2,1)}) fusion(bf16[16,96]{1,0:T(8,128)(2,1)S(1)} %select_reduce_fusion, bf16[16,128,2048]{2,1,0:T(8,128)(2,1)} %bitcast.50, s32[16,128]{1,0:T(8,128)S(1)} %broadcast_add_fusion, pred[16,128]{1,0:T(8,128)(4,1)S(1)} %bitcast.54), kind=kOutput, calls=%fused_computation.15 | convolution fusion | flops 811991040 | bytes 20984832 | tf_op jit(solution)/shard_map/sjt,std->sjd/dot_general | solution.py:80
  132.4 5.6 %fusion.6 = bf16[768,2048]{0,1:T(8,128)(2,1)S(1)} fusion(bf16[1536,2048]{1,0:T(8,128)(2,1)S(1)} %bitcast.52, bf16[1,1,1536,768]{3,2,1,0:T(8,128)(2,1)S(1)} %copy-done.2), kind=kOutput, calls=%fused_computation.16 | convolution fusion | flops 4833411072 | bytes 11796480 | tf_op jit(solution)/shard_map/dot_general | solution.py:122
  138.0 3.0 copy.86
  142.4 1.6 copy.79
  144.0 1.6 copy.81
  145.5 1.6 copy.80
  147.1 4.5 %reduce-scatter.4.cloned.1.call-done = bf16[384,2048]{1,0:T(8,128)(2,1)} async-done(((bf16[768,2048]{1,0:T(8,128)(2,1)}), bf16[384,2048]{1,0:T(8,128)(2,1)}) %reduce-scatter.4.cloned.1.call-update) | async-done | bytes 1572880
  151.6 2.6 copy.87
  154.2 5.5 %fusion.8 = (bf16[384,2048]{0,1:T(8,128)(2,1)S(1)}, bf16[384,2048]{0,1:T(8,128)(2,1)}, bf16[384,2048]{0,1:T(8,128)(2,1)}) fusion(bf16[384,2048]{0,1:T(8,128)(2,1)} %copy.87, bf16[1,384,2048]{1,2,0:T(8,128)(2,1)} %copy.81, bf16[1,384,2048]{1,2,0:T(8,128)(2,1)} %copy.80, bf16[1,384,2048]{1,2,0:T(8,128)(2,1)S(1)} %copy-done.1), kind=kLoop, calls=%fused_computation.18 | loop fusion | flops 15728640 | bytes 11010048 | tf_op jit(solution)/shard_map/convert_element_type | solution.py:29
  161.8 2.4 collective-permute-start.3
  164.2 4.3 %copy.73 = bf16[1,1,1536,768]{2,3,1,0:T(8,128)(2,1)} copy(bf16[1,1,1536,768]{3,2,1,0:T(8,128)(2,1)} %param.11) | data formatting | bytes 4718592 | tf_op args[3]
  168.7 1.5 collective-permute-start
  170.8 26.4 %collective-permute-done.1 = bf16[384,2048]{0,1:T(8,128)(2,1)S(1)} collective-permute-done((bf16[384,2048]{0,1:T(8,128)(2,1)}, bf16[384,2048]{0,1:T(8,128)(2,1)S(1)}, u32[]{:S(2)}, u32[]{:S(2)}) %collective-permute-start.1) | collective-permute-done | bytes 1572896 | tf_op jit(solution)/shard_map/ppermute | solution.py:145
  197.5 32.9 %collective-permute-done.2 = bf16[384,2048]{0,1:T(8,128)(2,1)} collective-permute-done((bf16[384,2048]{0,1:T(8,128)(2,1)}, bf16[384,2048]{0,1:T(8,128)(2,1)}, u32[]{:S(2)}, u32[]{:S(2)}) %collective-permute-start.2) | collective-permute-done | bytes 1572896 | tf_op jit(solution)/shard_map/ppermute | solution.py:145
  230.4 4.0 %collective-permute-start.7 = (bf16[384,2048]{0,1:T(8,128)(2,1)}, bf16[384,2048]{0,1:T(8,128)(2,1)}, u32[]{:S(2)}, u32[]{:S(2)}) collective-permute-start(bf16[384,2048]{0,1:T(8,128)(2,1)} %get-tuple-element.28), channel_id=1, source_target_pairs={{0,8},{1,9},{2,10},{3,11},{4,12},{5,13},{6,14},{7,15},{8,0},{9,1},... | collective-permute-start | bytes 4718600 | tf_op jit(solution)/shard_map/ppermute | solution.py:145
  235.8 8.5 %multiply_reduce_fusion = f32[1536]{0:T(1024)S(1)} fusion(bf16[1536,2048]{1,0:T(8,128)(2,1)} %bitcast.51, bf16[1,768,2048]{2,1,0:T(8,128)(2,1)} %all-gather.6.cloned.1.call-done, bf16[1,1,1536,768]{2,3,1,0:T(8,128)(2,1)} %copy.73), kind=kOutput, calls=%fused_computation.3 | convolution fusion | flops 4835375616 | bytes 11802624 | tf_op jit(solution)/shard_map/dot_general | solution.py:114
  245.1 3.7 all-to-all-start
  252.1 49.8 %all-to-all-done = f32[16,1,96]{2,1,0:T(1,128)S(1)} async-done(((f32[16,1,96]{2,1,0:T(1,128)}), f32[16,1,96]{2,1,0:T(1,128)S(1)}, u32[]{:S(2)}, u32[]{:S(2)}) %all-to-all-start) | async-done | bytes 6176 | tf_op jit(solution)/shard_map/all_to_all | solution.py:129
  303.1 6.1 %gather_fusion = f32[1024]{0:T(1024)S(1)} fusion(f32[1536]{0:T(1024)S(1)} %reshape.67, s32[1024]{0:T(1024)S(1)} %broadcast_clamp_fusion), kind=kCustom, calls=%fused_computation | custom fusion | bytes 12288 | tf_op jit(solution)/shard_map/gather | solution.py:132
  309.5 1.5 collective-permute-start.9
  315.3 2.7 select_bitcast_fusion.2
  318.0 1.6 copy.83
  319.7 2.7 select_bitcast_fusion.1
  322.4 1.6 copy.84
  324.0 19.9 %collective-permute-done.9 = bf16[384,2048]{0,1:T(8,128)(2,1)} collective-permute-done((bf16[384,2048]{0,1:T(8,128)(2,1)S(1)}, bf16[384,2048]{0,1:T(8,128)(2,1)}, u32[]{:S(2)}, u32[]{:S(2)}) %collective-permute-start.9) | collective-permute-done | bytes 1572896 | tf_op jit(solution)/shard_map/ppermute | solution.py:145
  343.9 32.6 %collective-permute-done.10 = bf16[384,2048]{0,1:T(8,128)(2,1)} collective-permute-done((bf16[384,2048]{0,1:T(8,128)(2,1)S(1)}, bf16[384,2048]{0,1:T(8,128)(2,1)}, u32[]{:S(2)}, u32[]{:S(2)}) %collective-permute-start.10) | collective-permute-done | bytes 1572896 | tf_op jit(solution)/shard_map/ppermute | solution.py:145
  376.5 2.4 collective-permute-done.11
  378.9 2.3 select_bitcast_fusion
  381.2 1.6 copy.85
  (73 shorter events, 16.7 us)
Async XLA Ops:
  7.2 117.2 %all-gather.4.cloned.1.call-start = ((), (), s32[]{:S(2)}) async-start(), calls=%async_computation.2 | async-start | bytes 8912896 | tf_op jit(solution)/shard_map/all_gather | solution.py:70
  7.9 143.7 %reduce-scatter.4.cloned.1.call-start = ((), (), s32[]{:S(2)}) async-start(), calls=%async_computation.4 | async-start | bytes 4718592
  9.8 7.2 %copy-start.6 = (s32[128,8]{0,1:T(8,128)S(1)}, s32[128,8]{0,1:T(8,128)}, u32[]{:S(2)}) copy-start(s32[128,8]{0,1:T(8,128)} %param.9) | copy-start | bytes 12292
  9.8 7.2 %copy-start.7 = (f32[128,8]{0,1:T(8,128)S(1)}, f32[128,8]{0,1:T(8,128)}, u32[]{:S(2)}) copy-start(f32[128,8]{0,1:T(8,128)} %param.10) | copy-start | bytes 12292
  124.4 8.0 %copy-start.2 = (bf16[1,1,1536,768]{3,2,1,0:T(8,128)(2,1)S(1)}, bf16[1,1,1536,768]{3,2,1,0:T(8,128)(2,1)}, u32[]{:S(2)}) copy-start(bf16[1,1,1536,768]{3,2,1,0:T(8,128)(2,1)} %param.11) | copy-start | bytes 7077892
  141.0 1.4 copy-start
  141.0 94.9 %all-gather.6.cloned.1.call-start = ((), (), s32[]{:S(2)}) async-start(), calls=%async_computation.3 | async-start | bytes 4718592 | tf_op jit(solution)/shard_map/all_gather | solution.py:54
  142.4 1.6 copy-start.4
  144.0 1.6 copy-start.5
  147.1 7.1 %copy-start.1 = (bf16[1,384,2048]{1,2,0:T(8,128)(2,1)S(1)}, bf16[1,384,2048]{1,2,0:T(8,128)(2,1)}, u32[]{:S(2)}) copy-start(bf16[1,384,2048]{1,2,0:T(8,128)(2,1)} %copy.79) | copy-start | bytes 4718596
  159.8 37.4 %collective-permute-start.1 = (bf16[384,2048]{0,1:T(8,128)(2,1)}, bf16[384,2048]{0,1:T(8,128)(2,1)S(1)}, u32[]{:S(2)}, u32[]{:S(2)}) collective-permute-start(bf16[384,2048]{0,1:T(8,128)(2,1)} %get-tuple-element.27), channel_id=1, source_target_pairs={{0,2},{1,3},{2,0},{3,1},{4,6},{5,7},{6,4},{7,5},{8,10},{9,11},{10,... | collective-permute-start | bytes 4718600 | tf_op jit(solution)/shard_map/ppermute | solution.py:145
  161.2 69.1 %collective-permute-start.2 = (bf16[384,2048]{0,1:T(8,128)(2,1)}, bf16[384,2048]{0,1:T(8,128)(2,1)}, u32[]{:S(2)}, u32[]{:S(2)}) collective-permute-start(bf16[384,2048]{0,1:T(8,128)(2,1)} %get-tuple-element.27), channel_id=1, source_target_pairs={{0,4},{1,5},{2,6},{3,7},{4,0},{5,1},{6,2},{7,3},{8,12},{9,13},{10,... | collective-permute-start | bytes 4718600 | tf_op jit(solution)/shard_map/ppermute | solution.py:145
  161.8 72.6 %collective-permute-start.3 = (bf16[384,2048]{0,1:T(8,128)(2,1)}, bf16[384,2048]{0,1:T(8,128)(2,1)}, u32[]{:S(2)}, u32[]{:S(2)}) collective-permute-start(bf16[384,2048]{0,1:T(8,128)(2,1)} %get-tuple-element.27), channel_id=1, source_target_pairs={{0,8},{1,9},{2,10},{3,11},{4,12},{5,13},{6,14},{7,15},{8,0},{9,1},... | collective-permute-start | bytes 4718600 | tf_op jit(solution)/shard_map/ppermute | solution.py:145
  168.7 140.8 %collective-permute-start = (bf16[384,2048]{0,1:T(8,128)(2,1)}, bf16[384,2048]{0,1:T(8,128)(2,1)}, u32[]{:S(2)}, u32[]{:S(2)}) collective-permute-start(bf16[384,2048]{0,1:T(8,128)(2,1)} %get-tuple-element.27), channel_id=1, source_target_pairs={{0,1},{1,0},{2,3},{3,2},{4,5},{5,4},{6,7},{7,6},{8,9},{9,8},{10,11... | collective-permute-start | bytes 4718600 | tf_op jit(solution)/shard_map/ppermute | solution.py:145
  170.2 140.8 %collective-permute-start.5 = (bf16[384,2048]{0,1:T(8,128)(2,1)}, bf16[384,2048]{0,1:T(8,128)(2,1)}, u32[]{:S(2)}, u32[]{:S(2)}) collective-permute-start(bf16[384,2048]{0,1:T(8,128)(2,1)} %get-tuple-element.28), channel_id=1, source_target_pairs={{0,2},{1,3},{2,0},{3,1},{4,6},{5,7},{6,4},{7,5},{8,10},{9,11},{10,... | collective-permute-start | bytes 4718600 | tf_op jit(solution)/shard_map/ppermute | solution.py:145
  197.2 47.2 %copy-start.3 = (bf16[384,2048]{0,1:T(8,128)(2,1)}, bf16[384,2048]{0,1:T(8,128)(2,1)S(1)}, u32[]{:S(2)}) copy-start(bf16[384,2048]{0,1:T(8,128)(2,1)S(1)} %collective-permute-done.1) | copy-start | bytes 4718596
  197.2 115.3 %collective-permute-start.6 = (bf16[384,2048]{0,1:T(8,128)(2,1)}, bf16[384,2048]{0,1:T(8,128)(2,1)}, u32[]{:S(2)}, u32[]{:S(2)}) collective-permute-start(bf16[384,2048]{0,1:T(8,128)(2,1)} %get-tuple-element.28), channel_id=1, source_target_pairs={{0,4},{1,5},{2,6},{3,7},{4,0},{5,1},{6,2},{7,3},{8,12},{9,13},{10,... | collective-permute-start | bytes 4718600 | tf_op jit(solution)/shard_map/ppermute | solution.py:145
  230.4 83.6 %collective-permute-start.7 = (bf16[384,2048]{0,1:T(8,128)(2,1)}, bf16[384,2048]{0,1:T(8,128)(2,1)}, u32[]{:S(2)}, u32[]{:S(2)}) collective-permute-start(bf16[384,2048]{0,1:T(8,128)(2,1)} %get-tuple-element.28), channel_id=1, source_target_pairs={{0,8},{1,9},{2,10},{3,11},{4,12},{5,13},{6,14},{7,15},{8,0},{9,1},... | collective-permute-start | bytes 4718600 | tf_op jit(solution)/shard_map/ppermute | solution.py:145
  234.4 85.3 %collective-permute-start.4 = (bf16[384,2048]{0,1:T(8,128)(2,1)}, bf16[384,2048]{0,1:T(8,128)(2,1)}, u32[]{:S(2)}, u32[]{:S(2)}) collective-permute-start(bf16[384,2048]{0,1:T(8,128)(2,1)} %get-tuple-element.28), channel_id=1, source_target_pairs={{0,1},{1,0},{2,3},{3,2},{4,5},{5,4},{6,7},{7,6},{8,9},{9,8},{10,11... | collective-permute-start | bytes 4718600 | tf_op jit(solution)/shard_map/ppermute | solution.py:145
  235.8 12.9 %copy-start.8 = (s32[16]{0:T(128)S(1)}, s32[16]{0:T(128)}, u32[]{:S(2)}) copy-start(s32[16]{0:T(128)} %param.15) | copy-start | bytes 196
  245.1 56.8 %all-to-all-start = ((f32[16,1,96]{2,1,0:T(1,128)}), f32[16,1,96]{2,1,0:T(1,128)S(1)}, u32[]{:S(2)}, u32[]{:S(2)}) async-start(f32[16,1,96]{2,1,0:T(1,128)} %all_to_all.6), calls=%async_computation | async-start | bytes 16384 | tf_op jit(solution)/shard_map/all_to_all | solution.py:129
  309.5 34.4 %collective-permute-start.9 = (bf16[384,2048]{0,1:T(8,128)(2,1)S(1)}, bf16[384,2048]{0,1:T(8,128)(2,1)}, u32[]{:S(2)}, u32[]{:S(2)}) collective-permute-start(bf16[384,2048]{0,1:T(8,128)(2,1)S(1)} %get-tuple-element.26), channel_id=1, source_target_pairs={{0,2},{1,3},{2,0},{3,1},{4,6},{5,7},{6,4},{7,5},{8,10},{9,11},{10,... | collective-permute-start | bytes 4718600 | tf_op jit(solution)/shard_map/ppermute | solution.py:145
  311.0 65.5 %collective-permute-start.10 = (bf16[384,2048]{0,1:T(8,128)(2,1)S(1)}, bf16[384,2048]{0,1:T(8,128)(2,1)}, u32[]{:S(2)}, u32[]{:S(2)}) collective-permute-start(bf16[384,2048]{0,1:T(8,128)(2,1)S(1)} %get-tuple-element.26), channel_id=1, source_target_pairs={{0,4},{1,5},{2,6},{3,7},{4,0},{5,1},{6,2},{7,3},{8,12},{9,13},{10,... | collective-permute-start | bytes 4718600 | tf_op jit(solution)/shard_map/ppermute | solution.py:145
  312.5 66.4 %collective-permute-start.11 = (bf16[384,2048]{0,1:T(8,128)(2,1)S(1)}, bf16[384,2048]{0,1:T(8,128)(2,1)}, u32[]{:S(2)}, u32[]{:S(2)}) collective-permute-start(bf16[384,2048]{0,1:T(8,128)(2,1)S(1)} %get-tuple-element.26), channel_id=1, source_target_pairs={{0,8},{1,9},{2,10},{3,11},{4,12},{5,13},{6,14},{7,15},{8,0},{9,1},... | collective-permute-start | bytes 4718600 | tf_op jit(solution)/shard_map/ppermute | solution.py:145
  314.0 64.9 %collective-permute-start.8 = (bf16[384,2048]{0,1:T(8,128)(2,1)S(1)}, bf16[384,2048]{0,1:T(8,128)(2,1)}, u32[]{:S(2)}, u32[]{:S(2)}) collective-permute-start(bf16[384,2048]{0,1:T(8,128)(2,1)S(1)} %get-tuple-element.26), channel_id=1, source_target_pairs={{0,1},{1,0},{2,3},{3,2},{4,5},{5,4},{6,7},{7,6},{8,9},{9,8},{10,11... | collective-permute-start | bytes 4718600 | tf_op jit(solution)/shard_map/ppermute | solution.py:145
Sparse Core Ops, SparseCore 0:
  10.8 113.5 all-gather.3
  141.1 10.4 reduce-scatter.3
  153.3 13.2 all-gather.5

commit v2 on v1

--- a/solution.py
+++ b/solution.py
@@ -52,6 +52,23 @@
 
     weight = down_weight[0]
     weight_full = lax.all_gather(weight, "dp", axis=0, tiled=True)
+
+    mine = partner[me]
+    levels = axis_size.bit_length() - 1
+    which = jnp.int32(0)
+    for level in range(levels):
+        which = which + jnp.where(mine == (me ^ (1 << level)), level + 1, 0).astype(jnp.int32)
+
+    def relocate(arrays):
+        cases = [arrays]
+        for level in range(levels):
+            flip = 1 << level
+            cases.append(
+                lax.ppermute(arrays, "expert", perm=[(i, i ^ flip) for i in range(axis_size)])
+            )
+        return [lax.select_n(which, *[case[k] for case in cases]) for k in range(len(arrays))]
+
+    moved = relocate((weight, moment_one[0], moment_two[0]))
     hidden = saved_hidden[0, 0]
 
     prob_sum = jnp.sum(router_probs, axis=1, keepdims=True)
@@ -65,12 +82,16 @@
 
     gather_bytes = axis_size * tok_rows * width * grad_out.dtype.itemsize
     if gather_bytes <= gather_limit_bytes:
-        packed = jnp.concatenate([routes.astype(jnp.float32), router_probs], axis=1)
-        packed_all = lax.all_gather(packed, "expert", axis=0, tiled=True)
-        grad_all = lax.all_gather(grad_out, "expert", axis=0, tiled=True)
+        packed = jnp.concatenate([routes.astype(jnp.bfloat16), gate_low], axis=1)
+        extended = jnp.concatenate(
+            [grad_out, packed.reshape(-1, width).astype(grad_out.dtype)], axis=0
+        )
+        extended_all = lax.all_gather(extended, "expert", axis=0, tiled=False)
+        grad_all = extended_all[:, :tok_rows]
+        packed_all = extended_all[:, tok_rows:].reshape(axis_size * tok_rows, 2 * top_count)
+        grad_all, moved = lax.optimization_barrier((grad_all, moved))
         routes_all = packed_all[:, :top_count].astype(jnp.int32)
-        probs_all = packed_all[:, top_count:]
-        gate_all = (probs_all / jnp.sum(probs_all, axis=1, keepdims=True)).astype(jnp.bfloat16)
+        gate_all = packed_all[:, top_count:]
         hit_k = routes_all == me
         hit = jnp.any(hit_k, axis=1).reshape(axis_size, tok_rows)
         gate_tok = jnp.sum(
@@ -80,7 +101,7 @@
         dispatched = jnp.einsum(
             "sjt,std->sjd",
             onehot.astype(jnp.bfloat16),
-            grad_all.reshape(axis_size, tok_rows, width),
+            grad_all,
             preferred_element_type=jnp.float32,
         ).astype(jnp.bfloat16)
         slot_gate = jnp.sum(
@@ -125,29 +146,14 @@
         "dp",
         scatter_dimension=0,
         tiled=True,
-    ).astype(jnp.float32)
-    returned = lax.all_to_all(
-        products.reshape(axis_size, capacity), "expert", split_axis=0, concat_axis=0, tiled=True
     )
-    answer = returned.reshape(-1)[routes * capacity + pair_rank]
+    moved_grad = relocate((grad_sum,))
+    returned = lax.all_gather(products, "expert", axis=0, tiled=False)
+    answer = returned.reshape(-1)[routes * slot_count + me * capacity + pair_rank]
     gate_grad = (answer - jnp.sum(gate_share * answer, axis=1, keepdims=True)) / prob_sum
 
-    outputs = adam_update(weight, moment_one[0], moment_two[0], grad_sum)
-
-    mine = partner[me]
-    levels = axis_size.bit_length() - 1
-    which = jnp.int32(0)
-    cases = [outputs]
-    for level in range(levels):
-        flip = 1 << level
-        which = which + jnp.where(mine == (me ^ flip), level + 1, 0).astype(jnp.int32)
-        cases.append(
-            lax.ppermute(outputs, "expert", perm=[(i, i ^ flip) for i in range(axis_size)])
-        )
-    landed = [
-        lax.select_n(which, *[case[index] for case in cases]) for index in range(3)
-    ]
-    return (gate_grad, landed[0][None], landed[1][None], landed[2][None])
+    outputs = adam_update(moved[0], moved[1], moved[2], moved_grad[0].astype(jnp.float32))
+    return (gate_grad, outputs[0][None], outputs[1][None], outputs[2][None])
 
 
 def solution(mesh):

time: 394 us -> 494 us (1.25)
  blocking collectives: 36.1 us -> 78.2 us
  waiting for transfers between devices: 240 us -> 262 us
  starting transfers between devices: 21.3 us -> 34.1 us
  local copies, waits for them, and re-layouts: 36.5 us -> 47.1 us
  other arithmetic: 16.7 us -> 24.5 us
    ppermute x12 -> x16, waiting for transfers between devices: 114 us -> 247 us  [relocate(): lax.ppermute(arrays, 'expert', perm=[(i, i ^ flip) for i in range(axis_si...]
    all_gather x1, waiting for transfers between devices: 70.5 us -> 0.01 us  [on_device(): extended_all = lax.all_gather(extended, 'expert', axis=0, tiled=False)]
    all_to_all x1 -> x0, waiting for transfers between devices: 49.8 us -> none  [on_device(): lax.all_to_all(products.reshape(axis_size, capacity), 'expert', split_axi...]
    all_gather x1, blocking collectives: 36.1 us -> 78.2 us  [on_device(): returned = lax.all_gather(products, 'expert', axis=0, tiled=False)]
    ppermute x12 -> x16, starting transfers between devices: 17.3 us -> 33.8 us  [relocate(): lax.ppermute(arrays, 'expert', perm=[(i, i ^ flip) for i in range(axis_si...]
    select_n x1 -> x4, other arithmetic: 0.02 us -> 11.1 us  [the longest x3 11.1 us: relocate(): lax.select_n(which, *[case[k] for case in cases])]
    slice x0 -> x2, local copies, waits for them, and re-layouts: none -> 9.67 us  [the longest x1 8.3 us: on_device(): grad_all = extended_all[:, :tok_rows]]
    all_gather x1, waiting for transfers between devices: 0.01 us -> 7.12 us  [on_device(): weight_full = lax.all_gather(weight, 'dp', axis=0, tiled=True)]
  transfers between devices with their start and end apart: 16 -> 19, of which waited for: 8 -> 8; matrix products, arithmetic and copies ran while one was open for 14% -> 8% of each run, Pallas kernels for 0% -> 0%
where the time goes in v2:
time: 494 us; the launch traced here: 486 us
  waiting for transfers between devices  262 us (53%)
  blocking collectives  78.2 us (16%)
  local copies, waits for them, and re-layouts  47.1 us (10%)
  starting transfers between devices  34.1 us (7%)
  other arithmetic  24.5 us (5%)
  matrix products  23.3 us (5%)
  between operations  16.6 us (3%)
    ppermute x16, waiting for transfers between devices, relocate(): lax.ppermute(arrays, 'expert', perm=[(i, i ^ flip) for i in range(axis_si...  247 us
    all_gather x1, blocking collectives, on_device(): returned = lax.all_gather(products, 'expert', axis=0, tiled=False)  78.2 us
    ppermute x16, starting transfers between devices, relocate(): lax.ppermute(arrays, 'expert', perm=[(i, i ^ flip) for i in range(axis_si...  33.8 us
    unnamed x35, local copies, waits for them, and re-layouts  22.4 us
    select_n x3, other arithmetic, relocate(): lax.select_n(which, *[case[k] for case in cases])  11.1 us
  transfers between devices with their start and end apart: 19, of which 8 were waited for; matrix products, arithmetic and copies ran while one was open for 8% of the time, Pallas kernels for 0%

profile of v2, /device:TPU:8, one launch (start us, length us, event | category | flops | bytes accessed | tf_op | source)
XLA Modules:
  0.0 486.0 jit_solution(10784242169269261889)
XLA Ops:
  9.1 7.0 %gather_fusion.1 = s32[1024]{0:T(1024)S(1)} fusion(s32[128,16]{0,1:T(8,128)S(1)} %add_bitcast_fusion, s32[1024]{0:T(1024)S(1)} %reshape.69), kind=kCustom, calls=%fused_computation.1 | custom fusion | bytes 16384 | tf_op jit(solution)/shard_map/jit(take_along_axis)/gather | solution.py:81
  18.5 3.0 collective-permute-start.11
  24.6 2.6 copy.84
  27.7 87.3 %collective-permute-done.10 = bf16[384,2048]{0,1:T(8,128)(2,1)} collective-permute-done((bf16[384,2048]{0,1:T(8,128)(2,1)S(1)}, bf16[384,2048]{0,1:T(8,128)(2,1)}, u32[]{:S(2)}, u32[]{:S(2)}) %collective-permute-start.10) | collective-permute-done | bytes 1572896 | tf_op jit(solution)/shard_map/ppermute | solution.py:67
  114.9 2.8 collective-permute-start.5
  120.3 5.7 %collective-permute-start.7 = (bf16[384,2048]{0,1:T(8,128)(2,1)}, bf16[384,2048]{0,1:T(8,128)(2,1)}, u32[]{:S(2)}, u32[]{:S(2)}) collective-permute-start(bf16[384,2048]{0,1:T(8,128)(2,1)} %bitcast.51), channel_id=1, source_target_pairs={{0,8},{1,9},{2,10},{3,11},{4,12},{5,13},{6,14},{7,15},{8,0},{9,1},... | collective-permute-start | bytes 4718600 | tf_op jit(solution)/shard_map/ppermute | solution.py:67
  129.3 41.8 %collective-permute-done.5 = bf16[384,2048]{0,1:T(8,128)(2,1)} collective-permute-done((bf16[384,2048]{0,1:T(8,128)(2,1)}, bf16[384,2048]{0,1:T(8,128)(2,1)}, u32[]{:S(2)}, u32[]{:S(2)}) %collective-permute-start.5) | collective-permute-done | bytes 1572896 | tf_op jit(solution)/shard_map/ppermute | solution.py:67
  171.1 4.9 %collective-permute-start.2 = (bf16[384,2048]{0,1:T(8,128)(2,1)}, bf16[384,2048]{0,1:T(8,128)(2,1)}, u32[]{:S(2)}, u32[]{:S(2)}) collective-permute-start(bf16[384,2048]{0,1:T(8,128)(2,1)} %bitcast.54), channel_id=1, source_target_pairs={{0,4},{1,5},{2,6},{3,7},{4,0},{5,1},{6,2},{7,3},{8,12},{9,13},{10,... | collective-permute-start | bytes 4718600 | tf_op jit(solution)/shard_map/ppermute | solution.py:67
  176.0 62.4 %collective-permute-done.6 = bf16[384,2048]{0,1:T(8,128)(2,1)} collective-permute-done((bf16[384,2048]{0,1:T(8,128)(2,1)}, bf16[384,2048]{0,1:T(8,128)(2,1)}, u32[]{:S(2)}, u32[]{:S(2)}) %collective-permute-start.6) | collective-permute-done | bytes 1572896 | tf_op jit(solution)/shard_map/ppermute | solution.py:67
  238.4 4.9 %collective-permute-start.3 = (bf16[384,2048]{0,1:T(8,128)(2,1)}, bf16[384,2048]{0,1:T(8,128)(2,1)}, u32[]{:S(2)}, u32[]{:S(2)}) collective-permute-start(bf16[384,2048]{0,1:T(8,128)(2,1)} %bitcast.55), channel_id=1, source_target_pairs={{0,8},{1,9},{2,10},{3,11},{4,12},{5,13},{6,14},{7,15},{8,0},{9,1},... | collective-permute-start | bytes 4718600 | tf_op jit(solution)/shard_map/ppermute | solution.py:67
  246.6 2.9 select_select_fusion.1
  249.4 4.2 select_select_fusion.2
  253.6 49.6 %collective-permute-done.2 = bf16[384,2048]{0,1:T(8,128)(2,1)} collective-permute-done((bf16[384,2048]{0,1:T(8,128)(2,1)}, bf16[384,2048]{0,1:T(8,128)(2,1)}, u32[]{:S(2)}, u32[]{:S(2)}) %collective-permute-start.2) | collective-permute-done | bytes 1572896 | tf_op jit(solution)/shard_map/ppermute | solution.py:67
  303.2 4.9 %collective-permute-done.3 = bf16[384,2048]{0,1:T(8,128)(2,1)} collective-permute-done((bf16[384,2048]{0,1:T(8,128)(2,1)}, bf16[384,2048]{0,1:T(8,128)(2,1)}, u32[]{:S(2)}, u32[]{:S(2)}) %collective-permute-start.3) | collective-permute-done | bytes 1572896 | tf_op jit(solution)/shard_map/ppermute | solution.py:67
  308.1 4.0 select_select_fusion.3
  314.8 8.3 %slice.22 = bf16[16,128,2048]{2,1,0:T(8,128)(2,1)} slice(bf16[16,129,2048]{2,1,0:T(8,128)(2,1)} %all-gather.10.cloned.1.call-done), slice={[0:16], [0:128], [0:2048]} | slice | bytes 16777216 | tf_op jit(solution)/shard_map/slice | solution.py:90
  323.8 8.0 %broadcast_multiply_fusion = (bf16[16,96,2048]{2,1,0:T(8,128)(2,1)S(1)}, bf16[16,96,2048]{2,1,0:T(8,128)(2,1)}) fusion(bf16[16,96]{1,0:T(8,128)(2,1)S(1)} %select_reduce_fusion.1, bf16[16,128,2048]{2,1,0:T(8,128)(2,1)} %slice.22, s32[16,128]{1,0:T(8,128)S(1)} %broadcast_add_fusion, pred[16,128]{1,0:T(8,128)(4,1)S(1)} %bitcast.60), kind=kOutput, calls=%fused_computation.15 | convolution fusion | flops 811991040 | bytes 20984832 | tf_op jit(solution)/shard_map/sjt,std->sjd/dot_general | solution.py:101
  331.8 6.8 %fusion.6 = bf16[768,2048]{0,1:T(8,128)(2,1)} fusion(bf16[1536,2048]{1,0:T(8,128)(2,1)S(1)} %bitcast.57, bf16[1,1,1536,768]{3,2,1,0:T(8,128)(2,1)S(1)} %copy-done.6), kind=kOutput, calls=%fused_computation.16 | convolution fusion | flops 4833411072 | bytes 11796480 | tf_op jit(solution)/shard_map/dot_general | solution.py:143
  338.6 4.7 copy.94
  344.0 4.3 copy.80
  348.6 7.1 %reduce-scatter.4.cloned.1.call-done = bf16[384,2048]{1,0:T(8,128)(2,1)} async-done(((bf16[768,2048]{1,0:T(8,128)(2,1)}), bf16[384,2048]{1,0:T(8,128)(2,1)}) %reduce-scatter.4.cloned.1.call-update) | async-done | bytes 1572880
  355.7 1.9 copy.95
  361.1 2.4 collective-permute-start.15
  363.5 7.1 %all-gather.8.cloned.1.call-done = bf16[1,768,2048]{2,1,0:T(8,128)(2,1)} async-done(((bf16[1,384,2048]{2,1,0:T(8,128)(2,1)}), bf16[1,768,2048]{2,1,0:T(8,128)(2,1)}) %all-gather.8.cloned.1.call-update) | async-done | bytes 3145744 | tf_op jit(solution)/shard_map/all_gather | solution.py:54
  370.7 8.5 %multiply_reduce_fusion = f32[1536]{0:T(1024)S(1)} fusion(bf16[1536,2048]{1,0:T(8,128)(2,1)} %bitcast.56, bf16[1,768,2048]{2,1,0:T(8,128)(2,1)} %all-gather.8.cloned.1.call-done, bf16[1,1,1536,768]{2,3,1,0:T(8,128)(2,1)} %copy.80), kind=kOutput, calls=%fused_computation.3 | convolution fusion | flops 4835375616 | bytes 11802624 | tf_op jit(solution)/shard_map/dot_general | solution.py:135
  379.2 78.2 %all-gather.4 = f32[16,1,1536]{2,1,0:T(1,128)S(1)} all-gather(f32[1,1,1536]{2,1,0:T(1,128)S(1)} %reshape.88), channel_id=4, replica_groups=mesh['dp'=2,'expert'=16] {'expert'}, dimensions={0}, use_global_device_ids=true | all-gather | bytes 104448 | tf_op jit(solution)/shard_map/all_gather | solution.py:151
  457.4 6.1 %gather_fusion = f32[1024]{0:T(1024)S(1)} fusion(f32[24576]{0:T(1024)S(1)} %bitcast.43, s32[1024]{0:T(1024)S(1)} %broadcast_clamp_fusion), kind=kCustom, calls=%fused_computation | custom fusion | bytes 12288 | tf_op jit(solution)/shard_map/gather | solution.py:152
  464.6 5.2 %fusion.10 = (bf16[1,384,2048]{1,2,0:T(8,128)(2,1)}, bf16[384,2048]{0,1:T(8,128)(2,1)S(1)}) fusion(bf16[384,2048]{0,1:T(8,128)(2,1)S(1)} %select_select_fusion.1, bf16[384,2048]{0,1:T(8,128)(2,1)} %collective-permute-done.13, bf16[384,2048]{0,1:T(8,128)(2,1)} %collective-permute-done.14, bf16[384,2048]{0,1:T(8,128)(2,1)} %collective-permute-done.15, ...), kind=kLoop, calls=%fused_computation.20 | loop fusion | flops 8650752 | bytes 12582916 | tf_op jit(solution)/shard_map/broadcast_in_dim | solution.py:156
  469.8 3.9 fusion.11
  473.7 2.6 copy.91
  476.3 1.6 copy.92
  477.9 1.6 copy.93
  (88 shorter events, 23.0 us)
Async XLA Ops:
  7.2 305.0 %all-gather.10.cloned.1.call-start = ((), (), s32[]{:S(2)}) async-start(), calls=%async_computation.2 | async-start | bytes 9469952 | tf_op jit(solution)/shard_map/all_gather | solution.py:89
  9.1 7.2 %copy-start.10 = (f32[128,8]{0,1:T(8,128)S(1)}, f32[128,8]{0,1:T(8,128)}, u32[]{:S(2)}) copy-start(f32[128,8]{0,1:T(8,128)} %param.10) | copy-start | bytes 12292
  9.1 7.2 %copy-start.9 = (s32[128,8]{0,1:T(8,128)S(1)}, s32[128,8]{0,1:T(8,128)}, u32[]{:S(2)}) copy-start(s32[128,8]{0,1:T(8,128)} %param.9) | copy-start | bytes 12292
  9.1 7.5 %copy-start.8 = (bf16[128,2048]{1,0:T(8,128)(2,1)S(1)}, bf16[128,2048]{1,0:T(8,128)(2,1)}, u32[]{:S(2)}) copy-start(bf16[128,2048]{1,0:T(8,128)(2,1)} %param.8) | copy-start | bytes 1572868
  16.1 1.4 copy-start.7
  17.5 338.2 %reduce-scatter.4.cloned.1.call-start = ((), (), s32[]{:S(2)}) async-start(), calls=%async_computation.3 | async-start | bytes 4718592
  18.4 107.7 %copy-start.2 = (bf16[1,384,2048]{2,1,0:T(8,128)(2,1)S(1)}, bf16[1,384,2048]{2,1,0:T(8,128)(2,1)}, u32[]{:S(2)}) copy-start(bf16[1,384,2048]{2,1,0:T(8,128)(2,1)} %param.12) | copy-start | bytes 4718596
  18.4 96.5 %collective-permute-start.10 = (bf16[384,2048]{0,1:T(8,128)(2,1)S(1)}, bf16[384,2048]{0,1:T(8,128)(2,1)}, u32[]{:S(2)}, u32[]{:S(2)}) collective-permute-start(bf16[384,2048]{0,1:T(8,128)(2,1)S(1)} %bitcast.44), channel_id=1, source_target_pairs={{0,4},{1,5},{2,6},{3,7},{4,0},{5,1},{6,2},{7,3},{8,12},{9,13},{10,... | collective-permute-start | bytes 4718600 | tf_op jit(solution)/shard_map/ppermute | solution.py:67
  18.5 100.6 %collective-permute-start.11 = (bf16[384,2048]{0,1:T(8,128)(2,1)S(1)}, bf16[384,2048]{0,1:T(8,128)(2,1)}, u32[]{:S(2)}, u32[]{:S(2)}) collective-permute-start(bf16[384,2048]{0,1:T(8,128)(2,1)S(1)} %bitcast.45), channel_id=1, source_target_pairs={{0,8},{1,9},{2,10},{3,11},{4,12},{5,13},{6,14},{7,15},{8,0},{9,1},... | collective-permute-start | bytes 4718600 | tf_op jit(solution)/shard_map/ppermute | solution.py:67
  21.5 98.8 %collective-permute-start.8 = (bf16[384,2048]{0,1:T(8,128)(2,1)S(1)}, bf16[384,2048]{0,1:T(8,128)(2,1)}, u32[]{:S(2)}, u32[]{:S(2)}) collective-permute-start(bf16[384,2048]{0,1:T(8,128)(2,1)S(1)} %bitcast.46), channel_id=1, source_target_pairs={{0,1},{1,0},{2,3},{3,2},{4,5},{5,4},{6,7},{7,6},{8,9},{9,8},{10,11... | collective-permute-start | bytes 4718600 | tf_op jit(solution)/shard_map/ppermute | solution.py:67
  23.0 104.6 %collective-permute-start.9 = (bf16[384,2048]{0,1:T(8,128)(2,1)S(1)}, bf16[384,2048]{0,1:T(8,128)(2,1)}, u32[]{:S(2)}, u32[]{:S(2)}) collective-permute-start(bf16[384,2048]{0,1:T(8,128)(2,1)S(1)} %bitcast.47), channel_id=1, source_target_pairs={{0,2},{1,3},{2,0},{3,1},{4,6},{5,7},{6,4},{7,5},{8,10},{9,11},{10,... | collective-permute-start | bytes 4718600 | tf_op jit(solution)/shard_map/ppermute | solution.py:67
  27.1 216.2 %copy-start.11 = (s32[16]{0:T(128)S(1)}, s32[16]{0:T(128)}, u32[]{:S(2)}) copy-start(s32[16]{0:T(128)} %param.15) | copy-start | bytes 196
  27.1 102.0 %collective-permute-start.4 = (bf16[384,2048]{0,1:T(8,128)(2,1)}, bf16[384,2048]{0,1:T(8,128)(2,1)}, u32[]{:S(2)}, u32[]{:S(2)}) collective-permute-start(bf16[384,2048]{0,1:T(8,128)(2,1)} %bitcast.48), channel_id=1, source_target_pairs={{0,1},{1,0},{2,3},{3,2},{4,5},{5,4},{6,7},{7,6},{8,9},{9,8},{10,11... | collective-permute-start | bytes 4718600 | tf_op jit(solution)/shard_map/ppermute | solution.py:67
  114.9 56.1 %collective-permute-start.5 = (bf16[384,2048]{0,1:T(8,128)(2,1)}, bf16[384,2048]{0,1:T(8,128)(2,1)}, u32[]{:S(2)}, u32[]{:S(2)}) collective-permute-start(bf16[384,2048]{0,1:T(8,128)(2,1)} %bitcast.49), channel_id=1, source_target_pairs={{0,2},{1,3},{2,0},{3,1},{4,6},{5,7},{6,4},{7,5},{8,10},{9,11},{10,... | collective-permute-start | bytes 4718600 | tf_op jit(solution)/shard_map/ppermute | solution.py:67
  119.1 119.3 %collective-permute-start.6 = (bf16[384,2048]{0,1:T(8,128)(2,1)}, bf16[384,2048]{0,1:T(8,128)(2,1)}, u32[]{:S(2)}, u32[]{:S(2)}) collective-permute-start(bf16[384,2048]{0,1:T(8,128)(2,1)} %bitcast.50), channel_id=1, source_target_pairs={{0,4},{1,5},{2,6},{3,7},{4,0},{5,1},{6,2},{7,3},{8,12},{9,13},{10,... | collective-permute-start | bytes 4718600 | tf_op jit(solution)/shard_map/ppermute | solution.py:67
  120.3 129.1 %collective-permute-start.7 = (bf16[384,2048]{0,1:T(8,128)(2,1)}, bf16[384,2048]{0,1:T(8,128)(2,1)}, u32[]{:S(2)}, u32[]{:S(2)}) collective-permute-start(bf16[384,2048]{0,1:T(8,128)(2,1)} %bitcast.51), channel_id=1, source_target_pairs={{0,8},{1,9},{2,10},{3,11},{4,12},{5,13},{6,14},{7,15},{8,0},{9,1},... | collective-permute-start | bytes 4718600 | tf_op jit(solution)/shard_map/ppermute | solution.py:67
  127.7 125.9 %collective-permute-start = (bf16[384,2048]{0,1:T(8,128)(2,1)}, bf16[384,2048]{0,1:T(8,128)(2,1)}, u32[]{:S(2)}, u32[]{:S(2)}) collective-permute-start(bf16[384,2048]{0,1:T(8,128)(2,1)} %bitcast.52), channel_id=1, source_target_pairs={{0,1},{1,0},{2,3},{3,2},{4,5},{5,4},{6,7},{7,6},{8,9},{9,8},{10,11... | collective-permute-start | bytes 4718600 | tf_op jit(solution)/shard_map/ppermute | solution.py:67
  129.1 124.5 %collective-permute-start.1 = (bf16[384,2048]{0,1:T(8,128)(2,1)}, bf16[384,2048]{0,1:T(8,128)(2,1)}, u32[]{:S(2)}, u32[]{:S(2)}) collective-permute-start(bf16[384,2048]{0,1:T(8,128)(2,1)} %bitcast.53), channel_id=1, source_target_pairs={{0,2},{1,3},{2,0},{3,1},{4,6},{5,7},{6,4},{7,5},{8,10},{9,11},{10,... | collective-permute-start | bytes 4718600 | tf_op jit(solution)/shard_map/ppermute | solution.py:67
  171.1 132.1 %collective-permute-start.2 = (bf16[384,2048]{0,1:T(8,128)(2,1)}, bf16[384,2048]{0,1:T(8,128)(2,1)}, u32[]{:S(2)}, u32[]{:S(2)}) collective-permute-start(bf16[384,2048]{0,1:T(8,128)(2,1)} %bitcast.54), channel_id=1, source_target_pairs={{0,4},{1,5},{2,6},{3,7},{4,0},{5,1},{6,2},{7,3},{8,12},{9,13},{10,... | collective-permute-start | bytes 4718600 | tf_op jit(solution)/shard_map/ppermute | solution.py:67
  238.4 69.7 %collective-permute-start.3 = (bf16[384,2048]{0,1:T(8,128)(2,1)}, bf16[384,2048]{0,1:T(8,128)(2,1)}, u32[]{:S(2)}, u32[]{:S(2)}) collective-permute-start(bf16[384,2048]{0,1:T(8,128)(2,1)} %bitcast.55), channel_id=1, source_target_pairs={{0,8},{1,9},{2,10},{3,11},{4,12},{5,13},{6,14},{7,15},{8,0},{9,1},... | collective-permute-start | bytes 4718600 | tf_op jit(solution)/shard_map/ppermute | solution.py:67
  246.5 2.9 copy-start.3
  249.4 58.7 %copy-start.4 = (bf16[1,384,2048]{1,2,0:T(8,128)(2,1)S(1)}, bf16[1,384,2048]{1,2,0:T(8,128)(2,1)}, u32[]{:S(2)}) copy-start(bf16[1,384,2048]{1,2,0:T(8,128)(2,1)} %copy.83) | copy-start | bytes 4718596
  323.8 8.0 %copy-start.6 = (bf16[1,1,1536,768]{3,2,1,0:T(8,128)(2,1)S(1)}, bf16[1,1,1536,768]{3,2,1,0:T(8,128)(2,1)}, u32[]{:S(2)}) copy-start(bf16[1,1,1536,768]{3,2,1,0:T(8,128)(2,1)} %param.11) | copy-start | bytes 7077892
  343.3 27.4 %all-gather.8.cloned.1.call-start = ((), (), s32[]{:S(2)}) async-start(), calls=%async_computation.1 | async-start | bytes 4718592 | tf_op jit(solution)/shard_map/all_gather | solution.py:54
  357.6 107.0 %collective-permute-start.12 = (bf16[384,2048]{0,1:T(8,128)(2,1)S(1)}, bf16[384,2048]{0,1:T(8,128)(2,1)}, u32[]{:S(2)}, u32[]{:S(2)}) collective-permute-start(bf16[384,2048]{0,1:T(8,128)(2,1)S(1)} %copy.95), channel_id=1, source_target_pairs={{0,1},{1,0},{2,3},{3,2},{4,5},{5,4},{6,7},{7,6},{8,9},{9,8},{10,11... | collective-permute-start | bytes 4718600 | tf_op jit(solution)/shard_map/ppermute | solution.py:67
  359.1 105.5 %collective-permute-start.13 = (bf16[384,2048]{0,1:T(8,128)(2,1)S(1)}, bf16[384,2048]{0,1:T(8,128)(2,1)}, u32[]{:S(2)}, u32[]{:S(2)}) collective-permute-start(bf16[384,2048]{0,1:T(8,128)(2,1)S(1)} %copy.95), channel_id=1, source_target_pairs={{0,2},{1,3},{2,0},{3,1},{4,6},{5,7},{6,4},{7,5},{8,10},{9,11},{10,... | collective-permute-start | bytes 4718600 | tf_op jit(solution)/shard_map/ppermute | solution.py:67
  360.6 104.0 %collective-permute-start.14 = (bf16[384,2048]{0,1:T(8,128)(2,1)S(1)}, bf16[384,2048]{0,1:T(8,128)(2,1)}, u32[]{:S(2)}, u32[]{:S(2)}) collective-permute-start(bf16[384,2048]{0,1:T(8,128)(2,1)S(1)} %copy.95), channel_id=1, source_target_pairs={{0,4},{1,5},{2,6},{3,7},{4,0},{5,1},{6,2},{7,3},{8,12},{9,13},{10,... | collective-permute-start | bytes 4718600 | tf_op jit(solution)/shard_map/ppermute | solution.py:67
  361.1 103.5 %collective-permute-start.15 = (bf16[384,2048]{0,1:T(8,128)(2,1)S(1)}, bf16[384,2048]{0,1:T(8,128)(2,1)}, u32[]{:S(2)}, u32[]{:S(2)}) collective-permute-start(bf16[384,2048]{0,1:T(8,128)(2,1)S(1)} %copy.95), channel_id=1, source_target_pairs={{0,8},{1,9},{2,10},{3,11},{4,12},{5,13},{6,14},{7,15},{8,0},{9,1},... | collective-permute-start | bytes 4718600 | tf_op jit(solution)/shard_map/ppermute | solution.py:67
  464.6 5.3 %copy-start = (bf16[384,2048]{0,1:T(8,128)(2,1)S(1)}, bf16[384,2048]{0,1:T(8,128)(2,1)}, u32[]{:S(2)}) copy-start(bf16[384,2048]{0,1:T(8,128)(2,1)} %select_select_fusion.2) | copy-start | bytes 4718596
  464.6 5.3 %copy-start.1 = (bf16[384,2048]{0,1:T(8,128)(2,1)S(1)}, bf16[384,2048]{0,1:T(8,128)(2,1)}, u32[]{:S(2)}) copy-start(bf16[384,2048]{0,1:T(8,128)(2,1)} %select_select_fusion.3) | copy-start | bytes 4718596
  476.3 1.6 copy-start.5
Sparse Core Ops, SparseCore 0:
  17.6 222.0 all-gather.9
  343.4 12.2 reduce-scatter.3
  357.3 13.2 all-gather.7

commit v3 on v2

--- a/solution.py
+++ b/solution.py
@@ -53,22 +53,6 @@
     weight = down_weight[0]
     weight_full = lax.all_gather(weight, "dp", axis=0, tiled=True)
 
-    mine = partner[me]
-    levels = axis_size.bit_length() - 1
-    which = jnp.int32(0)
-    for level in range(levels):
-        which = which + jnp.where(mine == (me ^ (1 << level)), level + 1, 0).astype(jnp.int32)
-
-    def relocate(arrays):
-        cases = [arrays]
-        for level in range(levels):
-            flip = 1 << level
-            cases.append(
-                lax.ppermute(arrays, "expert", perm=[(i, i ^ flip) for i in range(axis_size)])
-            )
-        return [lax.select_n(which, *[case[k] for case in cases]) for k in range(len(arrays))]
-
-    moved = relocate((weight, moment_one[0], moment_two[0]))
     hidden = saved_hidden[0, 0]
 
     prob_sum = jnp.sum(router_probs, axis=1, keepdims=True)
@@ -89,7 +73,6 @@
         extended_all = lax.all_gather(extended, "expert", axis=0, tiled=False)
         grad_all = extended_all[:, :tok_rows]
         packed_all = extended_all[:, tok_rows:].reshape(axis_size * tok_rows, 2 * top_count)
-        grad_all, moved = lax.optimization_barrier((grad_all, moved))
         routes_all = packed_all[:, :top_count].astype(jnp.int32)
         gate_all = packed_all[:, top_count:]
         hit_k = routes_all == me
@@ -147,13 +130,50 @@
         scatter_dimension=0,
         tiled=True,
     )
-    moved_grad = relocate((grad_sum,))
     returned = lax.all_gather(products, "expert", axis=0, tiled=False)
     answer = returned.reshape(-1)[routes * slot_count + me * capacity + pair_rank]
     gate_grad = (answer - jnp.sum(gate_share * answer, axis=1, keepdims=True)) / prob_sum
 
-    outputs = adam_update(moved[0], moved[1], moved[2], moved_grad[0].astype(jnp.float32))
-    return (gate_grad, outputs[0][None], outputs[1][None], outputs[2][None])
+    outputs = adam_update(weight, moment_one[0], moment_two[0], grad_sum.astype(jnp.float32))
+    outputs, gate_grad = lax.optimization_barrier((outputs, gate_grad))
+
+    mine = partner[me]
+    levels = axis_size.bit_length() - 1
+    device_iota = jnp.arange(expert_count, dtype=jnp.int32)
+    which = jnp.int32(0)
+    level_mask = jnp.int32(0)
+    for level in range(levels):
+        which = which + jnp.where(mine == (me ^ (1 << level)), level + 1, 0).astype(jnp.int32)
+        used = jnp.any(partner == (device_iota ^ (1 << level)))
+        level_mask = level_mask + jnp.where(used, 1 << level, 0).astype(jnp.int32)
+
+    def exchange(chosen):
+        def run(arrays):
+            cases = [arrays]
+            index = jnp.int32(0)
+            for position, level in enumerate(chosen):
+                flip = 1 << level
+                cases.append(
+                    lax.ppermute(arrays, "expert", perm=[(i, i ^ flip) for i in range(axis_size)])
+                )
+                index = index + jnp.where(which == level + 1, position + 1, 0).astype(jnp.int32)
+            if len(cases) == 1:
+                return arrays
+            return tuple(
+                lax.select_n(index, *[case[k] for case in cases]) for k in range(len(arrays))
+            )
+
+        return run
+
+    if levels <= 4:
+        branches = [
+            exchange([level for level in range(levels) if mask >> level & 1])
+            for mask in range(1 << levels)
+        ]
+        landed = lax.switch(level_mask, branches, outputs)
+    else:
+        landed = exchange(list(range(levels)))(outputs)
+    return (gate_grad, landed[0][None], landed[1][None], landed[2][None])
 
 
 def solution(mesh):

time: 494 us -> 358 us (0.72)
  waiting for transfers between devices: 262 us -> 181 us
  blocking collectives: 78.2 us -> 33.6 us
  loops' own time: 0 us -> 14.4 us
  starting transfers between devices: 34.1 us -> 24.8 us
  local copies, waits for them, and re-layouts: 47.1 us -> 38.8 us
    ppermute x16 -> x9, waiting for transfers between devices: 247 us -> 63.7 us  [run(): lax.ppermute(arrays, 'expert', perm=[(i, i ^ flip) for i in range(axis_si...]
    all_gather x1, waiting for transfers between devices: 0.01 us -> 117 us  [on_device(): extended_all = lax.all_gather(extended, 'expert', axis=0, tiled=False)]
    all_gather x1, blocking collectives: 78.2 us -> 33.6 us  [on_device(): returned = lax.all_gather(products, 'expert', axis=0, tiled=False)]
    another operation x0 -> x1, loops' own time: none -> 14.4 us  [on_device(): landed = lax.switch(level_mask, branches, outputs)]
    select_n x3 -> x0, other arithmetic: 11.1 us -> none  [relocate(): lax.select_n(which, *[case[k] for case in cases])]
    ppermute x16 -> x9, starting transfers between devices: 33.8 us -> 24.7 us  [run(): lax.ppermute(arrays, 'expert', perm=[(i, i ^ flip) for i in range(axis_si...]
    slice x1 -> x0, local copies, waits for them, and re-layouts: 8.3 us -> none  [on_device(): grad_all = extended_all[:, :tok_rows]]
    all_gather x1, waiting for transfers between devices: 7.12 us -> 0.02 us  [on_device(): weight_full = lax.all_gather(weight, 'dp', axis=0, tiled=True)]
  transfers between devices with their start and end apart: 19 -> 12, of which waited for: 8 -> 5; matrix products, arithmetic and copies ran while one was open for 8% -> 16% of each run, Pallas kernels for 0% -> 0%
where the time goes in v3:
time: 358 us; the launch traced here: 352 us
  waiting for transfers between devices  181 us (51%)
  local copies, waits for them, and re-layouts  38.8 us (11%)
  blocking collectives  33.6 us (9%)
  starting transfers between devices  24.8 us (7%)
  matrix products  21.6 us (6%)
  other arithmetic  20.6 us (6%)
  between operations  16.8 us (5%)
  loops' own time  14.4 us (4%)
    all_gather x1, waiting for transfers between devices, on_device(): extended_all = lax.all_gather(extended, 'expert', axis=0, tiled=False)  117 us
    ppermute x9, waiting for transfers between devices, run(): lax.ppermute(arrays, 'expert', perm=[(i, i ^ flip) for i in range(axis_si...  63.7 us
    all_gather x1, blocking collectives, on_device(): returned = lax.all_gather(products, 'expert', axis=0, tiled=False)  33.6 us
    ppermute x9, starting transfers between devices, run(): lax.ppermute(arrays, 'expert', perm=[(i, i ^ flip) for i in range(axis_si...  24.7 us
    unnamed x24, local copies, waits for them, and re-layouts  16.6 us
    another operation x1, loops' own time, on_device(): landed = lax.switch(level_mask, branches, outputs)  14.4 us
    broadcast_in_dim x3, other arithmetic, on_device(): return (gate_grad, landed[0][None], landed[1][None], landed[2][None])  10 us
    dot_general x1, matrix products, on_device(): lax.dot_general(dispatched, weight_full, (((1,), (1,)), ((), ())), prefer...  8.17 us
  transfers between devices with their start and end apart: 12, of which 5 were waited for; matrix products, arithmetic and copies ran while one was open for 16% of the time, Pallas kernels for 0%

profile of v3, /device:TPU:8, one launch (start us, length us, event | category | flops | bytes accessed | tf_op | source)
XLA Modules:
  0.0 352.1 jit_solution(15118360176340398092)
XLA Ops:
  9.1 7.0 %gather_fusion.1 = s32[1024]{0:T(1024)S(1)} fusion(s32[128,16]{0,1:T(8,128)S(1)} %add_bitcast_fusion, s32[1024]{0:T(1024)S(1)} %reshape.75), kind=kCustom, calls=%fused_computation.1 | custom fusion | bytes 16384 | tf_op jit(solution)/shard_map/jit(take_along_axis)/gather | solution.py:65
  16.6 0.9 maximum_bitcast_fusion
  18.3 116.9 %all-gather.10.cloned.1.call-done = bf16[16,129,2048]{2,1,0:T(8,128)(2,1)} async-done(((bf16[1,129,2048]{2,1,0:T(8,128)(2,1)}), bf16[16,129,2048]{2,1,0:T(8,128)(2,1)}) %all-gather.10.cloned.1.call-update) | async-done | bytes 8454160 | tf_op jit(solution)/shard_map/all_gather | solution.py:73
  135.2 1.4 slice_reduce_fusion
  138.6 7.9 %broadcast_multiply_fusion = (bf16[16,96,2048]{2,1,0:T(8,128)(2,1)S(1)}, bf16[16,96,2048]{2,1,0:T(8,128)(2,1)}) fusion(bf16[16,96]{1,0:T(8,128)(2,1)S(1)} %select_reduce_fusion.1, bf16[16,129,2048]{2,1,0:T(8,128)(2,1)} %all-gather.10.cloned.1.call-done, s32[16,128]{1,0:T(8,128)S(1)} %broadcast_add_fusion, pred[16,128]{1,0:T(8,128)(4,1)S(1)} %bitcast.157), kind=kOutput, calls=%fused_computation.62 | convolution fusion | flops 811991040 | bytes 20984832 | tf_op jit(solution)/shard_map/sjt,std->sjd/dot_general | solution.py:84
  146.4 5.6 %fusion.11 = bf16[768,2048]{0,1:T(8,128)(2,1)S(1)} fusion(bf16[1536,2048]{1,0:T(8,128)(2,1)S(1)} %bitcast.154, bf16[1,1,1536,768]{3,2,1,0:T(8,128)(2,1)S(1)} %copy-done.12), kind=kOutput, calls=%fused_computation.63 | convolution fusion | flops 4833411072 | bytes 11796480 | tf_op jit(solution)/shard_map/dot_general | solution.py:126
  152.0 3.0 copy.320
  155.1 4.4 %copy.265 = bf16[1,1,1536,768]{2,3,1,0:T(8,128)(2,1)} copy(bf16[1,1,1536,768]{3,2,1,0:T(8,128)(2,1)} %param.27) | data formatting | bytes 4718592 | tf_op args[3]
  159.5 1.6 copy.261
  161.4 1.6 copy.262
  162.9 2.8 copy.266
  169.0 8.2 %multiply_reduce_fusion = f32[1536]{0:T(1024)S(1)} fusion(bf16[1536,2048]{1,0:T(8,128)(2,1)} %bitcast.153, bf16[1,768,2048]{2,1,0:T(8,128)(2,1)} %all-gather.8.cloned.1.call-done, bf16[1,1,1536,768]{2,3,1,0:T(8,128)(2,1)S(1)} %copy-done.13), kind=kOutput, calls=%fused_computation.50 | convolution fusion | flops 4835375616 | bytes 11802624 | tf_op jit(solution)/shard_map/dot_general | solution.py:118
  177.2 33.6 %all-gather.4 = f32[16,1,1536]{2,1,0:T(1,128)S(1)} all-gather(f32[1,1,1536]{2,1,0:T(1,128)S(1)} %reshape.95), channel_id=4, replica_groups=mesh['dp'=2,'expert'=16] {'expert'}, dimensions={0}, use_global_device_ids=true | all-gather | bytes 104448 | tf_op jit(solution)/shard_map/all_gather | solution.py:133
  210.9 6.1 %gather_fusion = f32[1024]{0:T(1024)S(1)} fusion(f32[24576]{0:T(1024)S(1)} %bitcast.152, s32[1024]{0:T(1024)S(1)} %broadcast_clamp_fusion), kind=kCustom, calls=%fused_computation | custom fusion | bytes 12288 | tf_op jit(solution)/shard_map/gather | solution.py:134
  217.4 2.6 copy.321
  220.0 5.5 %fusion.13 = (bf16[384,2048]{0,1:T(8,128)(2,1)S(1)}, bf16[384,2048]{0,1:T(8,128)(2,1)S(1)}, bf16[384,2048]{0,1:T(8,128)(2,1)}) fusion(bf16[384,2048]{0,1:T(8,128)(2,1)} %copy.321, bf16[1,384,2048]{1,2,0:T(8,128)(2,1)} %copy.266, bf16[1,384,2048]{1,2,0:T(8,128)(2,1)} %copy.262, bf16[1,384,2048]{1,2,0:T(8,128)(2,1)} %copy.261), kind=kLoop, calls=%fused_computation.65 | loop fusion | flops 15728640 | bytes 11010048 | tf_op jit(solution)/shard_map/convert_element_type | solution.py:29
  226.1 119.2 %conditional.1 = (bf16[1,384,2048]{2,1,0:T(8,128)(2,1)}, bf16[1,384,2048]{2,1,0:T(8,128)(2,1)}, bf16[1,384,2048]{2,1,0:T(8,128)(2,1)}) conditional(s32[]{:T(128)} %clamp.3, (bf16[384,2048]{0,1:T(8,128)(2,1)S(1)}, bf16[384,2048]{0,1:T(8,128)(2,1)}, bf16[384,2048]{0,1:T(8,128)(2,1)S(1)}) %tuple.297, (s32[]{:T(128)}, ...), branch_computations={%region_14.15_spmd, %region_15.16_spmd, %region_16.17_spmd, %regio... | conditional | flops 9437217 | bytes 132121528 | solution.py:173
  226.1 1.6 copy.294
  227.8 6.8 %collective-permute-start.35 = (bf16[384,2048]{1,0:T(8,128)(2,1)}, bf16[384,2048]{1,0:T(8,128)(2,1)}, u32[]{:S(2)}, u32[]{:S(2)}) collective-permute-start(bf16[384,2048]{1,0:T(8,128)(2,1)} %copy.294), channel_id=1, source_target_pairs={{0,4},{1,5},{2,6},{3,7},{4,0},{5,1},{6,2},{7,3},{8,12},{9,13},{10,... | collective-permute-start | bytes 4718600 | tf_op jit(solution)/shard_map/cond/branch_7_fun/ppermute | solution.py:157
  234.6 2.6 copy.293
  237.2 2.0 collective-permute-start.30
  239.2 2.0 collective-permute-start.31
  241.2 24.1 %collective-permute-done.33 = bf16[384,2048]{1,0:T(8,128)(2,1)S(1)} collective-permute-done((bf16[384,2048]{1,0:T(8,128)(2,1)}, bf16[384,2048]{1,0:T(8,128)(2,1)S(1)}, u32[]{:S(2)}, u32[]{:S(2)}) %collective-permute-start.33) | collective-permute-done | bytes 1572896 | tf_op jit(solution)/shard_map/cond/branch_7_fun/ppermute | solution.py:157
  265.3 6.8 %collective-permute-start.32 = (bf16[384,2048]{1,0:T(8,128)(2,1)}, bf16[384,2048]{1,0:T(8,128)(2,1)}, u32[]{:S(2)}, u32[]{:S(2)}) collective-permute-start(bf16[384,2048]{1,0:T(8,128)(2,1)} %copy.293), channel_id=1, source_target_pairs={{0,4},{1,5},{2,6},{3,7},{4,0},{5,1},{6,2},{7,3},{8,12},{9,13},{10,... | collective-permute-start | bytes 4718600 | tf_op jit(solution)/shard_map/cond/branch_7_fun/ppermute | solution.py:157
  272.2 1.6 copy.292
  273.9 25.2 %collective-permute-done.30 = bf16[384,2048]{1,0:T(8,128)(2,1)} collective-permute-done((bf16[384,2048]{1,0:T(8,128)(2,1)}, bf16[384,2048]{1,0:T(8,128)(2,1)}, u32[]{:S(2)}, u32[]{:S(2)}) %collective-permute-start.30) | collective-permute-done | bytes 1572896 | tf_op jit(solution)/shard_map/cond/branch_7_fun/ppermute | solution.py:157
  299.1 6.8 %collective-permute-start.29 = (bf16[384,2048]{1,0:T(8,128)(2,1)}, bf16[384,2048]{1,0:T(8,128)(2,1)}, u32[]{:S(2)}, u32[]{:S(2)}) collective-permute-start(bf16[384,2048]{1,0:T(8,128)(2,1)} %copy.292), channel_id=1, source_target_pairs={{0,4},{1,5},{2,6},{3,7},{4,0},{5,1},{6,2},{7,3},{8,12},{9,13},{10,... | collective-permute-start | bytes 4718600 | tf_op jit(solution)/shard_map/cond/branch_7_fun/ppermute | solution.py:157
  308.8 3.3 select_bitcast_fusion.18
  312.2 3.4 select_bitcast_fusion.19
  315.6 9.5 %collective-permute-done.27 = bf16[384,2048]{1,0:T(8,128)(2,1)} collective-permute-done((bf16[384,2048]{1,0:T(8,128)(2,1)}, bf16[384,2048]{1,0:T(8,128)(2,1)}, u32[]{:S(2)}, u32[]{:S(2)}) %collective-permute-start.27) | collective-permute-done | bytes 1572896 | tf_op jit(solution)/shard_map/cond/branch_7_fun/ppermute | solution.py:157
  325.1 4.9 %collective-permute-done.29 = bf16[384,2048]{1,0:T(8,128)(2,1)} collective-permute-done((bf16[384,2048]{1,0:T(8,128)(2,1)}, bf16[384,2048]{1,0:T(8,128)(2,1)}, u32[]{:S(2)}, u32[]{:S(2)}) %collective-permute-start.29) | collective-permute-done | bytes 1572896 | tf_op jit(solution)/shard_map/cond/branch_7_fun/ppermute | solution.py:157
  330.0 3.3 select_bitcast_fusion.20
  (72 shorter events, 7.8 us)
Async XLA Ops:
  7.2 128.1 %all-gather.10.cloned.1.call-start = ((), (), s32[]{:S(2)}) async-start(), calls=%async_computation.2 | async-start | bytes 9469952 | tf_op jit(solution)/shard_map/all_gather | solution.py:73
  9.1 7.2 %copy-start.22 = (f32[128,8]{0,1:T(8,128)S(1)}, f32[128,8]{0,1:T(8,128)}, u32[]{:S(2)}) copy-start(f32[128,8]{0,1:T(8,128)} %param.26) | copy-start | bytes 12292
  9.1 7.2 %copy-start.21 = (s32[128,8]{0,1:T(8,128)S(1)}, s32[128,8]{0,1:T(8,128)}, u32[]{:S(2)}) copy-start(s32[128,8]{0,1:T(8,128)} %param.25) | copy-start | bytes 12292
  9.1 7.5 %copy-start.20 = (bf16[128,2048]{1,0:T(8,128)(2,1)S(1)}, bf16[128,2048]{1,0:T(8,128)(2,1)}, u32[]{:S(2)}) copy-start(bf16[128,2048]{1,0:T(8,128)(2,1)} %param.24) | copy-start | bytes 1572868
  17.5 151.6 %all-gather.8.cloned.1.call-start = ((), (), s32[]{:S(2)}) async-start(), calls=%async_computation.1 | async-start | bytes 4718592 | tf_op jit(solution)/shard_map/all_gather | solution.py:54
  18.2 199.1 %reduce-scatter.4.cloned.1.call-start = ((), (), s32[]{:S(2)}) async-start(), calls=%async_computation.3 | async-start | bytes 4718592
  138.6 7.9 %copy-start.12 = (bf16[1,1,1536,768]{3,2,1,0:T(8,128)(2,1)S(1)}, bf16[1,1,1536,768]{3,2,1,0:T(8,128)(2,1)}, u32[]{:S(2)}) copy-start(bf16[1,1,1536,768]{3,2,1,0:T(8,128)(2,1)} %param.27) | copy-start | bytes 7077892
  155.1 4.4 %copy-start = (bf16[1,384,2048]{2,1,0:T(8,128)(2,1)S(1)}, bf16[1,384,2048]{2,1,0:T(8,128)(2,1)}, u32[]{:S(2)}) copy-start(bf16[1,384,2048]{2,1,0:T(8,128)(2,1)} %param.28) | copy-start | bytes 4718596
  159.5 1.9 copy-start.15
  162.9 2.8 copy-start.23
  162.9 6.1 %copy-start.13 = (bf16[1,1,1536,768]{2,3,1,0:T(8,128)(2,1)S(1)}, bf16[1,1,1536,768]{2,3,1,0:T(8,128)(2,1)}, u32[]{:S(2)}) copy-start(bf16[1,1,1536,768]{2,3,1,0:T(8,128)(2,1)} %copy.265) | copy-start | bytes 7077892
  227.8 37.5 %collective-permute-start.33 = (bf16[384,2048]{1,0:T(8,128)(2,1)}, bf16[384,2048]{1,0:T(8,128)(2,1)S(1)}, u32[]{:S(2)}, u32[]{:S(2)}) collective-permute-start(bf16[384,2048]{1,0:T(8,128)(2,1)} %copy.294), channel_id=1, source_target_pairs={{0,1},{1,0},{2,3},{3,2},{4,5},{5,4},{6,7},{7,6},{8,9},{9,8},{10,11... | collective-permute-start | bytes 4718600 | tf_op jit(solution)/shard_map/cond/branch_7_fun/ppermute | solution.py:157
  227.8 46.0 %collective-permute-start.34 = (bf16[384,2048]{1,0:T(8,128)(2,1)}, bf16[384,2048]{1,0:T(8,128)(2,1)}, u32[]{:S(2)}, u32[]{:S(2)}) collective-permute-start(bf16[384,2048]{1,0:T(8,128)(2,1)} %copy.294), channel_id=1, source_target_pairs={{0,2},{1,3},{2,0},{3,1},{4,6},{5,7},{6,4},{7,5},{8,10},{9,11},{10,... | collective-permute-start | bytes 4718600 | tf_op jit(solution)/shard_map/cond/branch_7_fun/ppermute | solution.py:157
  227.8 46.0 %collective-permute-start.35 = (bf16[384,2048]{1,0:T(8,128)(2,1)}, bf16[384,2048]{1,0:T(8,128)(2,1)}, u32[]{:S(2)}, u32[]{:S(2)}) collective-permute-start(bf16[384,2048]{1,0:T(8,128)(2,1)} %copy.294), channel_id=1, source_target_pairs={{0,4},{1,5},{2,6},{3,7},{4,0},{5,1},{6,2},{7,3},{8,12},{9,13},{10,... | collective-permute-start | bytes 4718600 | tf_op jit(solution)/shard_map/cond/branch_7_fun/ppermute | solution.py:157
  237.2 61.9 %collective-permute-start.30 = (bf16[384,2048]{1,0:T(8,128)(2,1)}, bf16[384,2048]{1,0:T(8,128)(2,1)}, u32[]{:S(2)}, u32[]{:S(2)}) collective-permute-start(bf16[384,2048]{1,0:T(8,128)(2,1)} %copy.293), channel_id=1, source_target_pairs={{0,1},{1,0},{2,3},{3,2},{4,5},{5,4},{6,7},{7,6},{8,9},{9,8},{10,11... | collective-permute-start | bytes 4718600 | tf_op jit(solution)/shard_map/cond/branch_7_fun/ppermute | solution.py:157
  239.2 72.9 %collective-permute-start.31 = (bf16[384,2048]{1,0:T(8,128)(2,1)}, bf16[384,2048]{1,0:T(8,128)(2,1)}, u32[]{:S(2)}, u32[]{:S(2)}) collective-permute-start(bf16[384,2048]{1,0:T(8,128)(2,1)} %copy.293), channel_id=1, source_target_pairs={{0,2},{1,3},{2,0},{3,1},{4,6},{5,7},{6,4},{7,5},{8,10},{9,11},{10,... | collective-permute-start | bytes 4718600 | tf_op jit(solution)/shard_map/cond/branch_7_fun/ppermute | solution.py:157
  265.3 6.9 %copy-start.16 = (bf16[384,2048]{1,0:T(8,128)(2,1)}, bf16[384,2048]{1,0:T(8,128)(2,1)S(1)}, u32[]{:S(2)}) copy-start(bf16[384,2048]{1,0:T(8,128)(2,1)S(1)} %collective-permute-done.33) | copy-start | bytes 4718596 | tf_op jit(solution)/shard_map/cond
  265.3 46.9 %collective-permute-start.32 = (bf16[384,2048]{1,0:T(8,128)(2,1)}, bf16[384,2048]{1,0:T(8,128)(2,1)}, u32[]{:S(2)}, u32[]{:S(2)}) collective-permute-start(bf16[384,2048]{1,0:T(8,128)(2,1)} %copy.293), channel_id=1, source_target_pairs={{0,4},{1,5},{2,6},{3,7},{4,0},{5,1},{6,2},{7,3},{8,12},{9,13},{10,... | collective-permute-start | bytes 4718600 | tf_op jit(solution)/shard_map/cond/branch_7_fun/ppermute | solution.py:157
  272.2 36.7 %copy-start.4 = (bf16[384,2048]{1,0:T(8,128)(2,1)S(1)}, bf16[384,2048]{1,0:T(8,128)(2,1)}, u32[]{:S(2)}) copy-start(bf16[384,2048]{1,0:T(8,128)(2,1)} %copy.294) | copy-start | bytes 4718596 | tf_op jit(solution)/shard_map/cond
  273.8 51.3 %collective-permute-start.27 = (bf16[384,2048]{1,0:T(8,128)(2,1)}, bf16[384,2048]{1,0:T(8,128)(2,1)}, u32[]{:S(2)}, u32[]{:S(2)}) collective-permute-start(bf16[384,2048]{1,0:T(8,128)(2,1)} %copy.292), channel_id=1, source_target_pairs={{0,1},{1,0},{2,3},{3,2},{4,5},{5,4},{6,7},{7,6},{8,9},{9,8},{10,11... | collective-permute-start | bytes 4718600 | tf_op jit(solution)/shard_map/cond/branch_7_fun/ppermute | solution.py:157
  273.8 51.3 %collective-permute-start.28 = (bf16[384,2048]{1,0:T(8,128)(2,1)}, bf16[384,2048]{1,0:T(8,128)(2,1)}, u32[]{:S(2)}, u32[]{:S(2)}) collective-permute-start(bf16[384,2048]{1,0:T(8,128)(2,1)} %copy.292), channel_id=1, source_target_pairs={{0,2},{1,3},{2,0},{3,1},{4,6},{5,7},{6,4},{7,5},{8,10},{9,11},{10,... | collective-permute-start | bytes 4718600 | tf_op jit(solution)/shard_map/cond/branch_7_fun/ppermute | solution.py:157
  299.1 30.8 %collective-permute-start.29 = (bf16[384,2048]{1,0:T(8,128)(2,1)}, bf16[384,2048]{1,0:T(8,128)(2,1)}, u32[]{:S(2)}, u32[]{:S(2)}) collective-permute-start(bf16[384,2048]{1,0:T(8,128)(2,1)} %copy.292), channel_id=1, source_target_pairs={{0,4},{1,5},{2,6},{3,7},{4,0},{5,1},{6,2},{7,3},{8,12},{9,13},{10,... | collective-permute-start | bytes 4718600 | tf_op jit(solution)/shard_map/cond/branch_7_fun/ppermute | solution.py:157
  312.2 17.8 %copy-start.8 = (bf16[384,2048]{1,0:T(8,128)(2,1)S(1)}, bf16[384,2048]{1,0:T(8,128)(2,1)}, u32[]{:S(2)}) copy-start(bf16[384,2048]{1,0:T(8,128)(2,1)} %copy.292) | copy-start | bytes 4718596 | tf_op jit(solution)/shard_map/cond
Sparse Core Ops, SparseCore 0:
  17.6 117.5 all-gather.9
  136.8 11.8 all-gather.7
  155.2 10.6 reduce-scatter.3

commit v4 on v1

--- a/solution.py
+++ b/solution.py
@@ -133,20 +133,15 @@
     gate_grad = (answer - jnp.sum(gate_share * answer, axis=1, keepdims=True)) / prob_sum
 
     outputs = adam_update(weight, moment_one[0], moment_two[0], grad_sum)
+    outputs, gate_grad = lax.optimization_barrier((outputs, gate_grad))
 
-    mine = partner[me]
-    levels = axis_size.bit_length() - 1
-    which = jnp.int32(0)
-    cases = [outputs]
-    for level in range(levels):
-        flip = 1 << level
-        which = which + jnp.where(mine == (me ^ flip), level + 1, 0).astype(jnp.int32)
-        cases.append(
-            lax.ppermute(outputs, "expert", perm=[(i, i ^ flip) for i in range(axis_size)])
-        )
-    landed = [
-        lax.select_n(which, *[case[index] for case in cases]) for index in range(3)
-    ]
+    rows = weight.shape[0]
+    lane = width // axis_size
+    stacked = jnp.stack(outputs).reshape(3, rows, axis_size, lane).transpose(2, 0, 1, 3)
+    outward = lax.all_to_all(stacked, "expert", split_axis=0, concat_axis=0, tiled=True)
+    turned = jnp.take(outward, partner, axis=0)
+    landed = lax.all_to_all(turned, "expert", split_axis=0, concat_axis=0, tiled=True)
+    landed = landed.transpose(1, 2, 0, 3).reshape(3, rows, width)
     return (gate_grad, landed[0][None], landed[1][None], landed[2][None])
 
 

time: 394 us -> 432 us (1.096)
  waiting for transfers between devices: 240 us -> 274 us
  local copies, waits for them, and re-layouts: 36.5 us -> 46.3 us
    all_to_all x0 -> x2, waiting for transfers between devices: none -> 202 us  [the longest x1 101 us: on_device(): lax.all_to_all(stacked, 'expert', split_axis=0, concat_axis=0, tiled=True)]
    ppermute x12 -> x0, waiting for transfers between devices: 114 us -> none  [on_device(): lax.ppermute(outputs, 'expert', perm=[(i, i ^ flip) for i in range(axis_s...]
    all_to_all x1, waiting for transfers between devices: 49.8 us -> 0.6 us  [on_device(): lax.all_to_all(products.reshape(axis_size, capacity), 'expert', split_axi...]
    ppermute x12 -> x0, starting transfers between devices: 17.3 us -> none  [on_device(): lax.ppermute(outputs, 'expert', perm=[(i, i ^ flip) for i in range(axis_s...]
    all_to_all x0 -> x2, starting transfers between devices: none -> 14.6 us  [the longest x1 8.11 us: on_device(): lax.all_to_all(turned, 'expert', split_axis=0, concat_axis=0, tiled=True)]
    broadcast_in_dim x3 -> x0, other arithmetic: 7.71 us -> none  [on_device(): return (gate_grad, landed[0][None], landed[1][None], landed[2][None])]
    gather x0 -> x1, local copies, waits for them, and re-layouts: none -> 5.72 us  [on_device(): turned = jnp.take(outward, partner, axis=0)]
    select_n x0 -> x2, other arithmetic: none -> 5.1 us  [on_device(): turned = jnp.take(outward, partner, axis=0)]
  transfers between devices with their start and end apart: 16 -> 6, of which waited for: 8 -> 4; matrix products, arithmetic and copies ran while one was open for 14% -> 12% of each run, Pallas kernels for 0% -> 0%
where the time goes in v4:
time: 432 us; the launch traced here: 429 us
  waiting for transfers between devices  274 us (63%)
  local copies, waits for them, and re-layouts  46.3 us (11%)
  blocking collectives  36 us (8%)
  matrix products  23.3 us (5%)
  starting transfers between devices  20.1 us (5%)
  other arithmetic  15.2 us (4%)
  between operations  14 us (3%)
    all_to_all x1, waiting for transfers between devices, on_device(): lax.all_to_all(stacked, 'expert', split_axis=0, concat_axis=0, tiled=True)  101 us
    all_to_all x1, waiting for transfers between devices, on_device(): lax.all_to_all(turned, 'expert', split_axis=0, concat_axis=0, tiled=True)  101 us
    all_gather x1, waiting for transfers between devices, on_device(): grad_all = lax.all_gather(grad_out, 'expert', axis=0, tiled=True)  70.2 us
    all_gather x1, blocking collectives, on_device(): packed_all = lax.all_gather(packed, 'expert', axis=0, tiled=True)  36 us
    unnamed x26, local copies, waits for them, and re-layouts  21.4 us
    dot_general x1, matrix products, on_device(): lax.dot_general(dispatched, weight_full, (((1,), (1,)), ((), ())), prefer...  9.68 us
  transfers between devices with their start and end apart: 6, of which 4 were waited for; matrix products, arithmetic and copies ran while one was open for 12% of the time, Pallas kernels for 0%

profile of v4, /device:TPU:8, one launch (start us, length us, event | category | flops | bytes accessed | tf_op | source)
XLA Modules:
  0.0 428.8 jit_solution(13422678240837481146)
XLA Ops:
  7.2 0.7 all-gather.4.cloned.1.call-update
  7.9 0.7 all-gather.6.cloned.1.call-update
  8.7 0.7 bitcast_or_fusion
  9.4 0.7 fusion.15
  10.6 7.0 %gather_fusion.2 = s32[1024]{0:T(1024)S(1)} fusion(s32[128,16]{0,1:T(8,128)S(1)} %add_bitcast_fusion, s32[1024]{0:T(1024)S(1)} %reshape.101), kind=kCustom, calls=%fused_computation.2 | custom fusion | bytes 16384 | tf_op jit(solution)/shard_map/jit(take_along_axis)/gather | solution.py:64
  17.8 36.0 %all_gather.9 = f32[2048,16]{0,1:T(8,128)S(1)} all-gather(f32[128,16]{0,1:T(8,128)S(1)} %pad_maximum_fusion), channel_id=1, replica_groups=mesh['dp'=2,'expert'=16] {'expert'}, dimensions={0}, use_global_device_ids=true | all-gather | bytes 139264 | tf_op jit(solution)/shard_map/all_gather | solution.py:69
  54.6 70.2 %all-gather.4.cloned.1.call-done = bf16[2048,2048]{1,0:T(8,128)(2,1)} async-done(((bf16[128,2048]{1,0:T(8,128)(2,1)}), bf16[2048,2048]{1,0:T(8,128)(2,1)}) %all-gather.4.cloned.1.call-update) | async-done | bytes 8388624 | tf_op jit(solution)/shard_map/all_gather | solution.py:70
  124.8 8.0 %broadcast_multiply_fusion = (bf16[16,96,2048]{2,1,0:T(8,128)(2,1)S(1)}, bf16[16,96,2048]{2,1,0:T(8,128)(2,1)}) fusion(bf16[16,96]{1,0:T(8,128)(2,1)S(1)} %select_reduce_fusion, bf16[16,128,2048]{2,1,0:T(8,128)(2,1)} %bitcast.58, s32[16,128]{1,0:T(8,128)S(1)} %broadcast_add_fusion, pred[16,128]{1,0:T(8,128)(4,1)S(1)} %bitcast.68), kind=kOutput, calls=%fused_computation.18 | convolution fusion | flops 811991040 | bytes 20984832 | tf_op jit(solution)/shard_map/sjt,std->sjd/dot_general | solution.py:80
  132.8 5.6 %fusion.6 = bf16[768,2048]{0,1:T(8,128)(2,1)S(1)} fusion(bf16[1536,2048]{1,0:T(8,128)(2,1)S(1)} %bitcast.63, bf16[1,1,1536,768]{3,2,1,0:T(8,128)(2,1)S(1)} %copy-done.2), kind=kOutput, calls=%fused_computation.19 | convolution fusion | flops 4833411072 | bytes 11796480 | tf_op jit(solution)/shard_map/dot_general | solution.py:122
  138.4 3.0 copy.95
  141.5 1.6 copy-done.3
  143.1 2.4 copy.81
  145.8 9.7 %multiply_reduce_fusion = f32[1536]{0:T(1024)S(1)} fusion(bf16[1536,2048]{1,0:T(8,128)(2,1)} %bitcast.62, bf16[1,768,2048]{2,1,0:T(8,128)(2,1)} %all-gather.6.cloned.1.call-done, bf16[1,1,1536,768]{2,3,1,0:T(8,128)(2,1)} %copy.81), kind=kOutput, calls=%fused_computation.5 | convolution fusion | flops 4835375616 | bytes 11802624 | tf_op jit(solution)/shard_map/dot_general | solution.py:114
  155.5 0.7 all_to_all.12
  156.2 5.5 %all-to-all-start = ((f32[16,1,96]{2,1,0:T(1,128)}), f32[16,1,96]{2,1,0:T(1,128)S(1)}, u32[]{:S(2)}, u32[]{:S(2)}) async-start(f32[16,1,96]{2,1,0:T(1,128)} %all_to_all.12), calls=%async_computation | async-start | bytes 16384 | tf_op jit(solution)/shard_map/all_to_all | solution.py:129
  161.7 0.9 copy.79
  162.7 2.7 copy.80
  165.3 1.6 copy.82
  168.8 6.1 %gather_fusion = f32[1024]{0:T(1024)S(1)} fusion(f32[1536]{0:T(1024)S(1)} %reshape.83, s32[1024]{0:T(1024)S(1)} %broadcast_clamp_fusion), kind=kCustom, calls=%fused_computation | custom fusion | bytes 12288 | tf_op jit(solution)/shard_map/gather | solution.py:132
  175.3 2.7 copy.96
  178.0 4.2 fusion.8
  182.2 2.5 maximum_bitcast_fusion
  184.7 6.5 %all-to-all-start.1 = ((bf16[16,3,384,128]{2,3,1,0:T(8,128)(2,1)}), bf16[16,3,384,128]{2,3,1,0:T(8,128)(2,1)}, u32[]{:S(2)}, u32[]{:S(2)}) async-start(bf16[16,3,384,128]{2,3,1,0:T(8,128)(2,1)} %maximum_bitcast_fusion), calls=%async_computation.1 | async-start | bytes 9437184 | tf_op jit(solution)/shard_map/all_to_all | solution.py:141
  191.2 100.9 %all-to-all-done.1 = bf16[16,3,384,128]{2,3,1,0:T(8,128)(2,1)} async-done(((bf16[16,3,384,128]{2,3,1,0:T(8,128)(2,1)}), bf16[16,3,384,128]{2,3,1,0:T(8,128)(2,1)}, u32[]{:S(2)}, u32[]{:S(2)}) %all-to-all-start.1) | async-done | bytes 4718624 | tf_op jit(solution)/shard_map/all_to_all | solution.py:141
  292.1 5.7 %gather_fusion.1 = bf16[16,3,384,128]{2,3,1,0:T(8,128)(2,1)} fusion(bf16[16,3,384,128]{2,3,1,0:T(8,128)(2,1)} %all-to-all-done.1, s32[1024]{0:T(1024)S(1)} %pad_clamp_fusion), kind=kCustom, calls=%fused_computation.1 | custom fusion | bytes 9437248 | tf_op jit(solution)/shard_map/jit(_take)/gather | solution.py:142
  297.8 5.1 %broadcast_select_fusion = bf16[16,3,384,128]{2,3,1,0:T(8,128)(2,1)} fusion(bf16[16,3,384,128]{2,3,1,0:T(8,128)(2,1)} %gather_fusion.1, pred[16]{0:T(512)(128)(4,1)S(1)} %compare_and_fusion), kind=kLoop, calls=%fused_computation.6 | loop fusion | flops 2359296 | bytes 9437200 | tf_op jit(solution)/shard_map/jit(_take)/select_n | solution.py:142
  302.9 8.1 %all-to-all-start.2 = ((bf16[16,3,384,128]{2,3,1,0:T(8,128)(2,1)}), bf16[16,3,384,128]{2,3,1,0:T(8,128)(2,1)}, u32[]{:S(2)}, u32[]{:S(2)}) async-start(bf16[16,3,384,128]{2,3,1,0:T(8,128)(2,1)} %broadcast_select_fusion), calls=%async_computation.2 | async-start | bytes 9437184 | tf_op jit(solution)/shard_map/all_to_all | solution.py:143
  311.7 100.6 %all-to-all-done.2 = bf16[16,3,384,128]{2,3,1,0:T(8,128)(2,1)} async-done(((bf16[16,3,384,128]{2,3,1,0:T(8,128)(2,1)}), bf16[16,3,384,128]{2,3,1,0:T(8,128)(2,1)}, u32[]{:S(2)}, u32[]{:S(2)}) %all-to-all-start.2) | async-done | bytes 4718624 | tf_op jit(solution)/shard_map/all_to_all | solution.py:143
  412.3 4.1 fusion.17
  416.4 2.6 copy.92
  419.0 1.6 copy.93
  420.6 1.6 copy.94
  (54 shorter events, 4.8 us)
Async XLA Ops:
  7.2 117.6 %all-gather.4.cloned.1.call-start = ((), (), s32[]{:S(2)}) async-start(), calls=%async_computation.4 | async-start | bytes 8912896 | tf_op jit(solution)/shard_map/all_gather | solution.py:70
  7.9 137.9 %all-gather.6.cloned.1.call-start = ((), (), s32[]{:S(2)}) async-start(), calls=%async_computation.5 | async-start | bytes 4718592 | tf_op jit(solution)/shard_map/all_gather | solution.py:54
  8.6 166.6 %reduce-scatter.4.cloned.1.call-start = ((), (), s32[]{:S(2)}) async-start(), calls=%async_computation.6 | async-start | bytes 4718592
  10.6 7.2 %copy-start.5 = (s32[128,8]{0,1:T(8,128)S(1)}, s32[128,8]{0,1:T(8,128)}, u32[]{:S(2)}) copy-start(s32[128,8]{0,1:T(8,128)} %param.9) | copy-start | bytes 12292
  10.6 7.2 %copy-start.6 = (f32[128,8]{0,1:T(8,128)S(1)}, f32[128,8]{0,1:T(8,128)}, u32[]{:S(2)}) copy-start(f32[128,8]{0,1:T(8,128)} %param.10) | copy-start | bytes 12292
  124.8 8.0 %copy-start.2 = (bf16[1,1,1536,768]{3,2,1,0:T(8,128)(2,1)S(1)}, bf16[1,1,1536,768]{3,2,1,0:T(8,128)(2,1)}, u32[]{:S(2)}) copy-start(bf16[1,1,1536,768]{3,2,1,0:T(8,128)(2,1)} %param.11) | copy-start | bytes 7077892
  141.4 1.7 copy-start.3
  145.8 15.9 %copy-start = (bf16[1,384,2048]{2,1,0:T(8,128)(2,1)S(1)}, bf16[1,384,2048]{2,1,0:T(8,128)(2,1)}, u32[]{:S(2)}) copy-start(bf16[1,384,2048]{2,1,0:T(8,128)(2,1)} %param.12) | copy-start | bytes 4718596
  156.2 11.3 %all-to-all-start = ((f32[16,1,96]{2,1,0:T(1,128)}), f32[16,1,96]{2,1,0:T(1,128)S(1)}, u32[]{:S(2)}, u32[]{:S(2)}) async-start(f32[16,1,96]{2,1,0:T(1,128)} %all_to_all.12), calls=%async_computation | async-start | bytes 16384 | tf_op jit(solution)/shard_map/all_to_all | solution.py:129
  162.5 2.8 copy-start.4
  174.9 3.1 copy-start.1
  184.7 6.5 %copy-start.7 = (s32[16]{0:T(128)S(1)}, s32[16]{0:T(128)}, u32[]{:S(2)}) copy-start(s32[16]{0:T(128)} %param.15) | copy-start | bytes 196
  184.7 107.4 %all-to-all-start.1 = ((bf16[16,3,384,128]{2,3,1,0:T(8,128)(2,1)}), bf16[16,3,384,128]{2,3,1,0:T(8,128)(2,1)}, u32[]{:S(2)}, u32[]{:S(2)}) async-start(bf16[16,3,384,128]{2,3,1,0:T(8,128)(2,1)} %maximum_bitcast_fusion), calls=%async_computation.1 | async-start | bytes 9437184 | tf_op jit(solution)/shard_map/all_to_all | solution.py:141
  302.9 109.4 %all-to-all-start.2 = ((bf16[16,3,384,128]{2,3,1,0:T(8,128)(2,1)}), bf16[16,3,384,128]{2,3,1,0:T(8,128)(2,1)}, u32[]{:S(2)}, u32[]{:S(2)}) async-start(bf16[16,3,384,128]{2,3,1,0:T(8,128)(2,1)} %broadcast_select_fusion), calls=%async_computation.2 | async-start | bytes 9437184 | tf_op jit(solution)/shard_map/all_to_all | solution.py:143
Sparse Core Ops, SparseCore 0:
  10.8 113.9 all-gather.3
  126.4 11.7 all-gather.5
  141.6 10.8 reduce-scatter.3

commit v5 on v1

--- a/solution.py
+++ b/solution.py
@@ -132,7 +132,8 @@
     answer = returned.reshape(-1)[routes * capacity + pair_rank]
     gate_grad = (answer - jnp.sum(gate_share * answer, axis=1, keepdims=True)) / prob_sum
 
-    outputs = adam_update(weight, moment_one[0], moment_two[0], grad_sum)
+    outputs = jnp.stack(adam_update(weight, moment_one[0], moment_two[0], grad_sum))
+    outputs, gate_grad = lax.optimization_barrier((outputs, gate_grad))
 
     mine = partner[me]
     levels = axis_size.bit_length() - 1
@@ -144,9 +145,7 @@
         cases.append(
             lax.ppermute(outputs, "expert", perm=[(i, i ^ flip) for i in range(axis_size)])
         )
-    landed = [
-        lax.select_n(which, *[case[index] for case in cases]) for index in range(3)
-    ]
+    landed = lax.select_n(which, *cases)
     return (gate_grad, landed[0][None], landed[1][None], landed[2][None])
 
 

time: 394 us -> 413 us (1.048)
  waiting for transfers between devices: 240 us -> 269 us
  starting transfers between devices: 21.3 us -> 10.9 us
    ppermute x12 -> x4, waiting for transfers between devices: 114 us -> 197 us  [on_device(): lax.ppermute(outputs, 'expert', perm=[(i, i ^ flip) for i in range(axis_s...]
    all_to_all x1, waiting for transfers between devices: 49.8 us -> 0.58 us  [on_device(): lax.all_to_all(products.reshape(axis_size, capacity), 'expert', split_axi...]
    ppermute x12 -> x4, starting transfers between devices: 17.3 us -> 5.28 us  [on_device(): lax.ppermute(outputs, 'expert', perm=[(i, i ^ flip) for i in range(axis_s...]
    broadcast_in_dim x3 -> x0, other arithmetic: 7.71 us -> none  [on_device(): return (gate_grad, landed[0][None], landed[1][None], landed[2][None])]
    another operation x0 -> x2, other arithmetic: none -> 6.65 us  [on_device(): jnp.stack(adam_update(weight, moment_one[0], moment_two[0], grad_sum))]
    select_n x0 -> x1, other arithmetic: none -> 5.71 us  [on_device(): landed = lax.select_n(which, *cases)]
    convert_element_type x1 -> x0, other arithmetic: 5.54 us -> none  [adam_update(): second_new.astype(jnp.bfloat16)]
    unnamed x4, waiting for transfers between devices: 5.73 us -> 1.41 us
  transfers between devices with their start and end apart: 16 -> 8, of which waited for: 8 -> 5; matrix products, arithmetic and copies ran while one was open for 14% -> 13% of each run, Pallas kernels for 0% -> 0%
where the time goes in v5:
time: 413 us; the launch traced here: 410 us
  waiting for transfers between devices  269 us (65%)
  local copies, waits for them, and re-layouts  38.7 us (9%)
  blocking collectives  36 us (9%)
  matrix products  23.3 us (6%)
  between operations  16.6 us (4%)
  other arithmetic  15.8 us (4%)
  starting transfers between devices  10.9 us (3%)
    ppermute x4, waiting for transfers between devices, on_device(): lax.ppermute(outputs, 'expert', perm=[(i, i ^ flip) for i in range(axis_s...  197 us
    all_gather x1, waiting for transfers between devices, on_device(): grad_all = lax.all_gather(grad_out, 'expert', axis=0, tiled=True)  70.2 us
    all_gather x1, blocking collectives, on_device(): packed_all = lax.all_gather(packed, 'expert', axis=0, tiled=True)  36 us
    unnamed x26, local copies, waits for them, and re-layouts  21.4 us
    dot_general x1, matrix products, on_device(): lax.dot_general(dispatched, weight_full, (((1,), (1,)), ((), ())), prefer...  9.67 us
  transfers between devices with their start and end apart: 8, of which 5 were waited for; matrix products, arithmetic and copies ran while one was open for 13% of the time, Pallas kernels for 0%

profile of v5, /device:TPU:8, one launch (start us, length us, event | category | flops | bytes accessed | tf_op | source)
XLA Modules:
  0.0 410.0 jit_solution(17364676315170050839)
XLA Ops:
  7.9 0.7 all-gather.6.cloned.1.call-update
  8.7 0.7 fusion.18
  9.4 0.7 bitcast_or_fusion
  10.6 7.0 %gather_fusion.1 = s32[1024]{0:T(1024)S(1)} fusion(s32[128,16]{0,1:T(8,128)S(1)} %add_bitcast_fusion, s32[1024]{0:T(1024)S(1)} %reshape.77), kind=kCustom, calls=%fused_computation.1 | custom fusion | bytes 16384 | tf_op jit(solution)/shard_map/jit(take_along_axis)/gather | solution.py:64
  17.8 36.0 %all_gather.9 = f32[2048,16]{0,1:T(8,128)S(1)} all-gather(f32[128,16]{0,1:T(8,128)S(1)} %pad_maximum_fusion.1), channel_id=1, replica_groups=mesh['dp'=2,'expert'=16] {'expert'}, dimensions={0}, use_global_device_ids=true | all-gather | bytes 139264 | tf_op jit(solution)/shard_map/all_gather | solution.py:69
  54.6 70.2 %all-gather.4.cloned.1.call-done = bf16[2048,2048]{1,0:T(8,128)(2,1)} async-done(((bf16[128,2048]{1,0:T(8,128)(2,1)}), bf16[2048,2048]{1,0:T(8,128)(2,1)}) %all-gather.4.cloned.1.call-update) | async-done | bytes 8388624 | tf_op jit(solution)/shard_map/all_gather | solution.py:70
  124.8 8.0 %broadcast_multiply_fusion = (bf16[16,96,2048]{2,1,0:T(8,128)(2,1)S(1)}, bf16[16,96,2048]{2,1,0:T(8,128)(2,1)}) fusion(bf16[16,96]{1,0:T(8,128)(2,1)S(1)} %select_reduce_fusion, bf16[16,128,2048]{2,1,0:T(8,128)(2,1)} %bitcast.60, s32[16,128]{1,0:T(8,128)S(1)} %broadcast_add_fusion, pred[16,128]{1,0:T(8,128)(4,1)S(1)} %bitcast.64), kind=kOutput, calls=%fused_computation.17 | convolution fusion | flops 811991040 | bytes 20984832 | tf_op jit(solution)/shard_map/sjt,std->sjd/dot_general | solution.py:80
  132.9 5.6 %fusion.6 = bf16[768,2048]{0,1:T(8,128)(2,1)S(1)} fusion(bf16[1536,2048]{1,0:T(8,128)(2,1)S(1)} %bitcast.62, bf16[1,1,1536,768]{3,2,1,0:T(8,128)(2,1)S(1)} %copy-done.2), kind=kOutput, calls=%fused_computation.18 | convolution fusion | flops 4833411072 | bytes 11796480 | tf_op jit(solution)/shard_map/dot_general | solution.py:122
  138.4 3.0 copy.86
  141.5 1.6 copy-done.3
  143.1 2.4 copy.75
  145.8 9.7 %multiply_reduce_fusion = f32[1536]{0:T(1024)S(1)} fusion(bf16[1536,2048]{1,0:T(8,128)(2,1)} %bitcast.61, bf16[1,768,2048]{2,1,0:T(8,128)(2,1)} %all-gather.6.cloned.1.call-done, bf16[1,1,1536,768]{2,3,1,0:T(8,128)(2,1)} %copy.75), kind=kOutput, calls=%fused_computation.5 | convolution fusion | flops 4835375616 | bytes 11802624 | tf_op jit(solution)/shard_map/dot_general | solution.py:114
  156.2 5.5 %all-to-all-start = ((f32[16,1,96]{2,1,0:T(1,128)}), f32[16,1,96]{2,1,0:T(1,128)S(1)}, u32[]{:S(2)}, u32[]{:S(2)}) async-start(f32[16,1,96]{2,1,0:T(1,128)} %all_to_all.6), calls=%async_computation | async-start | bytes 16384 | tf_op jit(solution)/shard_map/all_to_all | solution.py:129
  161.7 0.9 copy.73
  162.6 2.7 copy.76
  165.3 1.6 copy.74
  168.8 6.1 %gather_fusion = f32[1024]{0:T(1024)S(1)} fusion(f32[1536]{0:T(1024)S(1)} %reshape.67, s32[1024]{0:T(1024)S(1)} %broadcast_clamp_fusion), kind=kCustom, calls=%fused_computation | custom fusion | bytes 12288 | tf_op jit(solution)/shard_map/gather | solution.py:132
  175.3 2.7 copy.87
  178.0 4.2 %fusion.12 = (bf16[1,384,2048]{1,2,0:T(8,128)(2,1)S(1)}, bf16[1,384,2048]{1,2,0:T(8,128)(2,1)S(1)}, bf16[1,384,2048]{1,2,0:T(8,128)(2,1)S(1)}) fusion(bf16[1,384,2048]{1,2,0:T(8,128)(2,1)S(1)} %copy-done.1, bf16[384,2048]{0,1:T(8,128)(2,1)} %copy.87, bf16[1,384,2048]{1,2,0:T(8,128)(2,1)} %copy.74, bf16[1,384,2048]{1,2,0:T(8,128)(2,1)S(1)} %copy.73), kind=kLoop, calls=%fused_computation.24 | loop fusion | flops 15728640 | bytes 11010048 | tf_op jit(solution)/shard_map/stack | solution.py:135
  182.2 2.5 pad_maximum_fusion
  184.6 0.9 collective-permute-start.1
  185.5 1.1 collective-permute-start.2
  186.7 1.8 collective-permute-start.3
  188.5 1.5 collective-permute-start
  193.8 93.2 %collective-permute-done.1 = bf16[3,384,2048]{1,2,0:T(8,128)(2,1)} collective-permute-done((bf16[3,384,2048]{1,2,0:T(8,128)(2,1)}, bf16[3,384,2048]{1,2,0:T(8,128)(2,1)}, u32[]{:S(2)}, u32[]{:S(2)}) %collective-permute-start.1) | collective-permute-done | bytes 4718624 | tf_op jit(solution)/shard_map/ppermute | solution.py:146
  287.0 100.2 %collective-permute-done.2 = bf16[3,384,2048]{1,2,0:T(8,128)(2,1)} collective-permute-done((bf16[3,384,2048]{1,2,0:T(8,128)(2,1)}, bf16[3,384,2048]{1,2,0:T(8,128)(2,1)}, u32[]{:S(2)}, u32[]{:S(2)}) %collective-permute-start.2) | collective-permute-done | bytes 4718624 | tf_op jit(solution)/shard_map/ppermute | solution.py:146
  387.2 3.1 collective-permute-done.3
  390.3 5.7 %select_select_fusion = bf16[3,384,2048]{1,2,0:T(8,128)(2,1)S(1)} fusion(bf16[3,384,2048]{1,2,0:T(8,128)(2,1)} %collective-permute-done.1, bf16[3,384,2048]{1,2,0:T(8,128)(2,1)} %collective-permute-done.2, bf16[3,384,2048]{1,2,0:T(8,128)(2,1)} %collective-permute-done.3, bf16[3,384,2048]{1,2,0:T(8,128)(2,1)} %pad_maximum_fusion, ...), kind=kLoop, calls=%fused_computation.4 | loop fusion | flops 9437184 | bytes 28311556 | tf_op jit(solution)/shard_map/select_n | solution.py:148
  396.0 1.6 fusion.20
  397.6 2.6 copy.83
  400.2 1.6 copy.84
  401.8 1.6 copy.85
  (55 shorter events, 6.7 us)
Async XLA Ops:
  7.2 117.7 %all-gather.4.cloned.1.call-start = ((), (), s32[]{:S(2)}) async-start(), calls=%async_computation.2 | async-start | bytes 8912896 | tf_op jit(solution)/shard_map/all_gather | solution.py:70
  7.9 137.9 %all-gather.6.cloned.1.call-start = ((), (), s32[]{:S(2)}) async-start(), calls=%async_computation.3 | async-start | bytes 4718592 | tf_op jit(solution)/shard_map/all_gather | solution.py:54
  8.6 166.6 %reduce-scatter.4.cloned.1.call-start = ((), (), s32[]{:S(2)}) async-start(), calls=%async_computation.4 | async-start | bytes 4718592
  10.6 7.2 %copy-start.5 = (s32[128,8]{0,1:T(8,128)S(1)}, s32[128,8]{0,1:T(8,128)}, u32[]{:S(2)}) copy-start(s32[128,8]{0,1:T(8,128)} %param.9) | copy-start | bytes 12292
  10.6 7.2 %copy-start.6 = (f32[128,8]{0,1:T(8,128)S(1)}, f32[128,8]{0,1:T(8,128)}, u32[]{:S(2)}) copy-start(f32[128,8]{0,1:T(8,128)} %param.10) | copy-start | bytes 12292
  124.8 8.0 %copy-start.2 = (bf16[1,1,1536,768]{3,2,1,0:T(8,128)(2,1)S(1)}, bf16[1,1,1536,768]{3,2,1,0:T(8,128)(2,1)}, u32[]{:S(2)}) copy-start(bf16[1,1,1536,768]{3,2,1,0:T(8,128)(2,1)} %param.11) | copy-start | bytes 7077892
  141.4 1.7 copy-start.3
  145.8 15.9 %copy-start = (bf16[1,384,2048]{2,1,0:T(8,128)(2,1)S(1)}, bf16[1,384,2048]{2,1,0:T(8,128)(2,1)}, u32[]{:S(2)}) copy-start(bf16[1,384,2048]{2,1,0:T(8,128)(2,1)} %param.12) | copy-start | bytes 4718596
  156.2 11.3 %all-to-all-start = ((f32[16,1,96]{2,1,0:T(1,128)}), f32[16,1,96]{2,1,0:T(1,128)S(1)}, u32[]{:S(2)}, u32[]{:S(2)}) async-start(f32[16,1,96]{2,1,0:T(1,128)} %all_to_all.6), calls=%async_computation | async-start | bytes 16384 | tf_op jit(solution)/shard_map/all_to_all | solution.py:129
  162.5 2.7 copy-start.4
  174.9 3.1 copy-start.1
  182.2 7.8 %copy-start.7 = (s32[16]{0:T(128)S(1)}, s32[16]{0:T(128)}, u32[]{:S(2)}) copy-start(s32[16]{0:T(128)} %param.15) | copy-start | bytes 196
  184.6 102.4 %collective-permute-start.1 = (bf16[3,384,2048]{1,2,0:T(8,128)(2,1)}, bf16[3,384,2048]{1,2,0:T(8,128)(2,1)}, u32[]{:S(2)}, u32[]{:S(2)}) collective-permute-start(bf16[3,384,2048]{1,2,0:T(8,128)(2,1)} %pad_maximum_fusion), channel_id=1, source_target_pairs={{0,2},{1,3},{2,0},{3,1},{4,6},{5,7},{6,4},{7,5},{8,10},{9,11},{10,... | collective-permute-start | bytes 14155784 | tf_op jit(solution)/shard_map/ppermute | solution.py:146
  185.5 201.6 %collective-permute-start.2 = (bf16[3,384,2048]{1,2,0:T(8,128)(2,1)}, bf16[3,384,2048]{1,2,0:T(8,128)(2,1)}, u32[]{:S(2)}, u32[]{:S(2)}) collective-permute-start(bf16[3,384,2048]{1,2,0:T(8,128)(2,1)} %pad_maximum_fusion), channel_id=1, source_target_pairs={{0,4},{1,5},{2,6},{3,7},{4,0},{5,1},{6,2},{7,3},{8,12},{9,13},{10,... | collective-permute-start | bytes 14155784 | tf_op jit(solution)/shard_map/ppermute | solution.py:146
  186.7 203.6 %collective-permute-start.3 = (bf16[3,384,2048]{1,2,0:T(8,128)(2,1)}, bf16[3,384,2048]{1,2,0:T(8,128)(2,1)}, u32[]{:S(2)}, u32[]{:S(2)}) collective-permute-start(bf16[3,384,2048]{1,2,0:T(8,128)(2,1)} %pad_maximum_fusion), channel_id=1, source_target_pairs={{0,8},{1,9},{2,10},{3,11},{4,12},{5,13},{6,14},{7,15},{8,0},{9,1},... | collective-permute-start | bytes 14155784 | tf_op jit(solution)/shard_map/ppermute | solution.py:146
  188.5 201.8 %collective-permute-start = (bf16[3,384,2048]{1,2,0:T(8,128)(2,1)}, bf16[3,384,2048]{1,2,0:T(8,128)(2,1)}, u32[]{:S(2)}, u32[]{:S(2)}) collective-permute-start(bf16[3,384,2048]{1,2,0:T(8,128)(2,1)} %pad_maximum_fusion), channel_id=1, source_target_pairs={{0,1},{1,0},{2,3},{3,2},{4,5},{5,4},{6,7},{7,6},{8,9},{9,8},{10,11... | collective-permute-start | bytes 14155784 | tf_op jit(solution)/shard_map/ppermute | solution.py:146
Sparse Core Ops, SparseCore 0:
  10.8 113.9 all-gather.3
  126.4 11.7 all-gather.5
  141.6 10.8 reduce-scatter.3

commit v6 on v5

--- a/solution.py
+++ b/solution.py
@@ -137,14 +137,33 @@
 
     mine = partner[me]
     levels = axis_size.bit_length() - 1
+    device_iota = jnp.arange(expert_count, dtype=jnp.int32)
     which = jnp.int32(0)
-    cases = [outputs]
     for level in range(levels):
+        which = which + jnp.where(mine == (me ^ (1 << level)), level + 1, 0).astype(jnp.int32)
+
+    def exchange(arrays, level):
         flip = 1 << level
-        which = which + jnp.where(mine == (me ^ flip), level + 1, 0).astype(jnp.int32)
-        cases.append(
-            lax.ppermute(outputs, "expert", perm=[(i, i ^ flip) for i in range(axis_size)])
-        )
+        return lax.ppermute(arrays, "expert", perm=[(i, i ^ flip) for i in range(axis_size)])
+
+    optional = list(range(max(levels - 2, 0), levels))
+    cases = [outputs] + [exchange(outputs, level) for level in range(levels - len(optional))]
+    if optional:
+        choice = jnp.int32(0)
+        for position, level in enumerate(optional):
+            used = jnp.any(partner == (device_iota ^ (1 << level)))
+            choice = choice + jnp.where(used, 1 << position, 0).astype(jnp.int32)
+
+        def branch(mask):
+            def run(arrays):
+                return tuple(
+                    exchange(arrays, level) if mask >> position & 1 else arrays
+                    for position, level in enumerate(optional)
+                )
+
+            return run
+
+        cases += list(lax.switch(choice, [branch(mask) for mask in range(1 << len(optional))], outputs))
     landed = lax.select_n(which, *cases)
     return (gate_grad, landed[0][None], landed[1][None], landed[2][None])
 

time: 413 us -> 339 us (0.82)
  waiting for transfers between devices: 269 us -> 169 us
  local copies, waits for them, and re-layouts: 38.7 us -> 66.3 us
    ppermute x4 -> x3, waiting for transfers between devices: 197 us -> 96.4 us  [exchange(): lax.ppermute(arrays, 'expert', perm=[(i, i ^ flip) for i in range(axis_si...]
    cond x0 -> x4, local copies, waits for them, and re-layouts: none -> 20.8 us  [the longest x2 13.3 us: on_device(): lax.switch(choice, [branch(mask) for mask in range(1 << len(optional))],...]
    optimization_barrier x0 -> x1, local copies, waits for them, and re-layouts: none -> 6.7 us  [on_device(): outputs, gate_grad = lax.optimization_barrier((outputs, gate_grad))]
  transfers between devices with their start and end apart: 8 -> 7, of which waited for: 5 -> 3; matrix products, arithmetic and copies ran while one was open for 13% -> 24% of each run, Pallas kernels for 0% -> 0%
where the time goes in v6:
time: 339 us; the launch traced here: 336 us
  waiting for transfers between devices  169 us (50%)
  local copies, waits for them, and re-layouts  66.3 us (20%)
  blocking collectives  36 us (11%)
  matrix products  23.3 us (7%)
  between operations  17.9 us (5%)
  other arithmetic  15.4 us (5%)
  starting transfers between devices  8.51 us (3%)
    ppermute x3, waiting for transfers between devices, exchange(): lax.ppermute(arrays, 'expert', perm=[(i, i ^ flip) for i in range(axis_si...  96.4 us
    all_gather x1, waiting for transfers between devices, on_device(): grad_all = lax.all_gather(grad_out, 'expert', axis=0, tiled=True)  70.2 us
    all_gather x1, blocking collectives, on_device(): packed_all = lax.all_gather(packed, 'expert', axis=0, tiled=True)  36 us
    unnamed x26, local copies, waits for them, and re-layouts  21.4 us
    cond x2, local copies, waits for them, and re-layouts, on_device(): lax.switch(choice, [branch(mask) for mask in range(1 << len(optional))],...  13.3 us
    dot_general x1, matrix products, on_device(): lax.dot_general(dispatched, weight_full, (((1,), (1,)), ((), ())), prefer...  9.68 us
    dot_general x1, matrix products, on_device(): jnp.einsum('sjt,std->sjd', onehot.astype(jnp.bfloat16), grad_all.reshape(...  8.03 us
    cond x2, local copies, waits for them, and re-layouts  7.49 us
  transfers between devices with their start and end apart: 7, of which 3 were waited for; matrix products, arithmetic and copies ran while one was open for 24% of the time, Pallas kernels for 0%

profile of v6, /device:TPU:8, one launch (start us, length us, event | category | flops | bytes accessed | tf_op | source)
XLA Modules:
  0.0 335.9 jit_solution(15761312047500023442)
XLA Ops:
  9.4 0.7 fusion.18
  10.6 7.0 %gather_fusion.1 = s32[1024]{0:T(1024)S(1)} fusion(s32[128,16]{0,1:T(8,128)S(1)} %add_bitcast_fusion, s32[1024]{0:T(1024)S(1)} %reshape.77), kind=kCustom, calls=%fused_computation.1 | custom fusion | bytes 16384 | tf_op jit(solution)/shard_map/jit(take_along_axis)/gather | solution.py:64
  17.8 36.0 %all_gather.9 = f32[2048,16]{0,1:T(8,128)S(1)} all-gather(f32[128,16]{0,1:T(8,128)S(1)} %pad_maximum_fusion.1), channel_id=1, replica_groups=mesh['dp'=2,'expert'=16] {'expert'}, dimensions={0}, use_global_device_ids=true | all-gather | bytes 139264 | tf_op jit(solution)/shard_map/all_gather | solution.py:69
  54.6 70.2 %all-gather.4.cloned.1.call-done = bf16[2048,2048]{1,0:T(8,128)(2,1)} async-done(((bf16[128,2048]{1,0:T(8,128)(2,1)}), bf16[2048,2048]{1,0:T(8,128)(2,1)}) %all-gather.4.cloned.1.call-update) | async-done | bytes 8388624 | tf_op jit(solution)/shard_map/all_gather | solution.py:70
  124.8 8.0 %broadcast_multiply_fusion = (bf16[16,96,2048]{2,1,0:T(8,128)(2,1)S(1)}, bf16[16,96,2048]{2,1,0:T(8,128)(2,1)}) fusion(bf16[16,96]{1,0:T(8,128)(2,1)S(1)} %select_reduce_fusion, bf16[16,128,2048]{2,1,0:T(8,128)(2,1)} %bitcast.60, s32[16,128]{1,0:T(8,128)S(1)} %broadcast_add_fusion, pred[16,128]{1,0:T(8,128)(4,1)S(1)} %bitcast.64), kind=kOutput, calls=%fused_computation.17 | convolution fusion | flops 811991040 | bytes 20984832 | tf_op jit(solution)/shard_map/sjt,std->sjd/dot_general | solution.py:80
  132.8 5.6 %fusion.6 = bf16[768,2048]{0,1:T(8,128)(2,1)S(1)} fusion(bf16[1536,2048]{1,0:T(8,128)(2,1)S(1)} %bitcast.62, bf16[1,1,1536,768]{3,2,1,0:T(8,128)(2,1)S(1)} %copy-done.2), kind=kOutput, calls=%fused_computation.18 | convolution fusion | flops 4833411072 | bytes 11796480 | tf_op jit(solution)/shard_map/dot_general | solution.py:122
  138.4 3.0 copy.116
  141.5 1.6 copy-done.3
  143.1 2.4 copy.99
  145.8 9.7 %multiply_reduce_fusion = f32[1536]{0:T(1024)S(1)} fusion(bf16[1536,2048]{1,0:T(8,128)(2,1)} %bitcast.61, bf16[1,768,2048]{2,1,0:T(8,128)(2,1)} %all-gather.6.cloned.1.call-done, bf16[1,1,1536,768]{2,3,1,0:T(8,128)(2,1)} %copy.99), kind=kOutput, calls=%fused_computation.5 | convolution fusion | flops 4835375616 | bytes 11802624 | tf_op jit(solution)/shard_map/dot_general | solution.py:114
  156.2 5.5 %all-to-all-start = ((f32[16,1,96]{2,1,0:T(1,128)}), f32[16,1,96]{2,1,0:T(1,128)S(1)}, u32[]{:S(2)}, u32[]{:S(2)}) async-start(f32[16,1,96]{2,1,0:T(1,128)} %all_to_all.6), calls=%async_computation | async-start | bytes 16384 | tf_op jit(solution)/shard_map/all_to_all | solution.py:129
  161.7 0.9 copy.97
  162.5 2.7 copy.100
  165.2 1.6 copy.98
  168.8 6.1 %gather_fusion = f32[1024]{0:T(1024)S(1)} fusion(f32[1536]{0:T(1024)S(1)} %reshape.67, s32[1024]{0:T(1024)S(1)} %broadcast_clamp_fusion), kind=kCustom, calls=%fused_computation | custom fusion | bytes 12288 | tf_op jit(solution)/shard_map/gather | solution.py:132
  175.3 2.7 copy.117
  178.0 4.2 %fusion.12 = (bf16[1,384,2048]{1,2,0:T(8,128)(2,1)S(1)}, bf16[1,384,2048]{1,2,0:T(8,128)(2,1)S(1)}, bf16[1,384,2048]{1,2,0:T(8,128)(2,1)S(1)}) fusion(bf16[1,384,2048]{1,2,0:T(8,128)(2,1)S(1)} %copy-done.1, bf16[384,2048]{0,1:T(8,128)(2,1)} %copy.117, bf16[1,384,2048]{1,2,0:T(8,128)(2,1)} %copy.98, bf16[1,384,2048]{1,2,0:T(8,128)(2,1)S(1)} %copy.97), kind=kLoop, calls=%fused_computation.24 | loop fusion | flops 15728640 | bytes 11010048 | tf_op jit(solution)/shard_map/stack | solution.py:135
  182.2 2.5 pad_maximum_fusion
  184.6 0.9 collective-permute-start.4
  185.5 1.5 collective-permute-start.5
  192.1 6.7 %copy.106 = bf16[3,384,2048]{2,1,0:T(8,128)(2,1)} copy(bf16[3,384,2048]{1,2,0:T(8,128)(2,1)} %pad_maximum_fusion) | data formatting | bytes 9437184 | tf_op jit(solution)/shard_map/optimization_barrier | solution.py:136
  198.8 104.4 %conditional.1 = (bf16[3,384,2048]{2,1,0:T(8,128)(2,1)}, bf16[3,384,2048]{2,1,0:T(8,128)(2,1)}) conditional(s32[]{:T(128)} %clamp.3, bf16[3,384,2048]{2,1,0:T(8,128)(2,1)} %copy.106, bf16[3,384,2048]{2,1,0:T(8,128)(2,1)} %copy.106, bf16[3,384,2048]{2,1,0:T(8,128)(2,1)} %copy.106, bf16[3,384,2048]{2,1,0:T(8,128)(2,1)} %copy.106), branch_computations={%region_13.14_spmd, %region_14.15_spmd, %region_15.16_spmd, %regio... | conditional | bytes 47186016 | solution.py:166
  199.4 5.3 %copy.121 = bf16[3,384,2048]{2,1,0:T(8,128)(2,1)} copy(bf16[3,384,2048]{2,1,0:T(8,128)(2,1)} %param.1) | data formatting | bytes 9437184 | tf_op jit(solution)/shard_map/cond
  204.7 96.4 %collective-permute-done = bf16[3,384,2048]{2,1,0:T(8,128)(2,1)S(1)} collective-permute-done((bf16[3,384,2048]{2,1,0:T(8,128)(2,1)}, bf16[3,384,2048]{2,1,0:T(8,128)(2,1)S(1)}, u32[]{:S(2)}, u32[]{:S(2)}) %collective-permute-start) | collective-permute-done | bytes 4718624 | tf_op jit(solution)/shard_map/cond/branch_1_fun/ppermute | solution.py:147
  301.1 2.2 copy.120
  303.3 6.7 %copy.110 = bf16[3,384,2048]{1,2,0:T(8,128)(2,1)} copy(bf16[3,384,2048]{2,1,0:T(8,128)(2,1)} %get-tuple-element.14) | data formatting | bytes 9437184 | tf_op jit(solution)/shard_map/cond | solution.py:166
  310.0 6.6 %copy.111 = bf16[3,384,2048]{1,2,0:T(8,128)(2,1)} copy(bf16[3,384,2048]{2,1,0:T(8,128)(2,1)} %get-tuple-element.15) | data formatting | bytes 9437184 | tf_op jit(solution)/shard_map/cond | solution.py:166
  317.3 4.7 %select_select_fusion = bf16[3,384,2048]{1,2,0:T(8,128)(2,1)S(1)} fusion(bf16[3,384,2048]{1,2,0:T(8,128)(2,1)} %collective-permute-done.5, bf16[3,384,2048]{1,2,0:T(8,128)(2,1)} %copy.110, bf16[3,384,2048]{1,2,0:T(8,128)(2,1)} %copy.111, bf16[3,384,2048]{1,2,0:T(8,128)(2,1)} %pad_maximum_fusion, bf16[3,384,2048]{1,2,0:T(8,128)(2,1)} %collective-permute-done.4, ...), kind=kLoop, calls=%fused_computation.4 | loop fusion | flops 9437184 | bytes 28311556 | tf_op jit(solution)/shard_map/select_n | solution.py:167
  322.0 1.6 fusion.20
  323.6 2.6 copy.113
  326.1 1.6 copy.114
  327.8 1.6 copy.115
  (60 shorter events, 9.3 us)
Async XLA Ops:
  7.2 117.6 %all-gather.4.cloned.1.call-start = ((), (), s32[]{:S(2)}) async-start(), calls=%async_computation.2 | async-start | bytes 8912896 | tf_op jit(solution)/shard_map/all_gather | solution.py:70
  7.9 137.9 %all-gather.6.cloned.1.call-start = ((), (), s32[]{:S(2)}) async-start(), calls=%async_computation.3 | async-start | bytes 4718592 | tf_op jit(solution)/shard_map/all_gather | solution.py:54
  8.6 166.6 %reduce-scatter.4.cloned.1.call-start = ((), (), s32[]{:S(2)}) async-start(), calls=%async_computation.4 | async-start | bytes 4718592
  10.6 7.2 %copy-start.5 = (s32[128,8]{0,1:T(8,128)S(1)}, s32[128,8]{0,1:T(8,128)}, u32[]{:S(2)}) copy-start(s32[128,8]{0,1:T(8,128)} %param.13) | copy-start | bytes 12292
  10.6 7.2 %copy-start.6 = (f32[128,8]{0,1:T(8,128)S(1)}, f32[128,8]{0,1:T(8,128)}, u32[]{:S(2)}) copy-start(f32[128,8]{0,1:T(8,128)} %param.14) | copy-start | bytes 12292
  124.8 8.0 %copy-start.2 = (bf16[1,1,1536,768]{3,2,1,0:T(8,128)(2,1)S(1)}, bf16[1,1,1536,768]{3,2,1,0:T(8,128)(2,1)}, u32[]{:S(2)}) copy-start(bf16[1,1,1536,768]{3,2,1,0:T(8,128)(2,1)} %param.15) | copy-start | bytes 7077892
  141.4 1.7 copy-start.3
  145.8 15.9 %copy-start = (bf16[1,384,2048]{2,1,0:T(8,128)(2,1)S(1)}, bf16[1,384,2048]{2,1,0:T(8,128)(2,1)}, u32[]{:S(2)}) copy-start(bf16[1,384,2048]{2,1,0:T(8,128)(2,1)} %param.16) | copy-start | bytes 4718596
  156.2 11.3 %all-to-all-start = ((f32[16,1,96]{2,1,0:T(1,128)}), f32[16,1,96]{2,1,0:T(1,128)S(1)}, u32[]{:S(2)}, u32[]{:S(2)}) async-start(f32[16,1,96]{2,1,0:T(1,128)} %all_to_all.6), calls=%async_computation | async-start | bytes 16384 | tf_op jit(solution)/shard_map/all_to_all | solution.py:129
  162.5 2.7 copy-start.4
  174.9 3.1 copy-start.1
  182.2 4.8 %copy-start.7 = (s32[16]{0:T(128)S(1)}, s32[16]{0:T(128)}, u32[]{:S(2)}) copy-start(s32[16]{0:T(128)} %param.19) | copy-start | bytes 196
  184.6 132.6 %collective-permute-start.4 = (bf16[3,384,2048]{1,2,0:T(8,128)(2,1)}, bf16[3,384,2048]{1,2,0:T(8,128)(2,1)}, u32[]{:S(2)}, u32[]{:S(2)}) collective-permute-start(bf16[3,384,2048]{1,2,0:T(8,128)(2,1)} %pad_maximum_fusion), channel_id=1, source_target_pairs={{0,1},{1,0},{2,3},{3,2},{4,5},{5,4},{6,7},{7,6},{8,9},{9,8},{10,11... | collective-permute-start | bytes 14155784 | tf_op jit(solution)/shard_map/ppermute | solution.py:147
  185.5 131.7 %collective-permute-start.5 = (bf16[3,384,2048]{1,2,0:T(8,128)(2,1)}, bf16[3,384,2048]{1,2,0:T(8,128)(2,1)}, u32[]{:S(2)}, u32[]{:S(2)}) collective-permute-start(bf16[3,384,2048]{1,2,0:T(8,128)(2,1)} %pad_maximum_fusion), channel_id=1, source_target_pairs={{0,2},{1,3},{2,0},{3,1},{4,6},{5,7},{6,4},{7,5},{8,10},{9,11},{10,... | collective-permute-start | bytes 14155784 | tf_op jit(solution)/shard_map/ppermute | solution.py:147
  198.8 102.3 %collective-permute-start = (bf16[3,384,2048]{2,1,0:T(8,128)(2,1)}, bf16[3,384,2048]{2,1,0:T(8,128)(2,1)S(1)}, u32[]{:S(2)}, u32[]{:S(2)}) collective-permute-start(bf16[3,384,2048]{2,1,0:T(8,128)(2,1)} %param.1), channel_id=1, source_target_pairs={{0,4},{1,5},{2,6},{3,7},{4,0},{5,1},{6,2},{7,3},{8,12},{9,13},{10,... | collective-permute-start | bytes 14155784 | tf_op jit(solution)/shard_map/cond/branch_1_fun/ppermute | solution.py:147
Sparse Core Ops, SparseCore 0:
  10.8 113.9 all-gather.3
  126.4 11.7 all-gather.5
  141.6 10.8 reduce-scatter.3
